TPU v7x, 32 devices: a whole 2x2x4 slice. The times are simulated.
32 devices in a mesh: req: 8 (over z, y), ep: 4 (over x, core).
Axes of the slice: x: 2, y: 2, z: 4, core: 2. Of those that a mesh axis runs over, the one named last changes fastest.
Arguments:
- tokens: bfloat16 [4096, 1536], P(('req', 'ep')), may hold values from -6 to 6
- seg_ids: int32 [4096], P(('req', 'ep')), may hold values from 0 to 3, never falling along the last dimension, each value on 1 to 2048 neighbouring positions
- routes: int32 [4096, 8], P(('req', 'ep')), may hold values from 0 to 39, all different within a row; in each aligned block of 128 rows (0 to 127, 128 to 255, ...) at most 48 rows name the same one
- route_weights: float32 [4096, 8], P(('req', 'ep')), may hold values from 0.05 to 0.3
- norm1_gain: float32 [1536], replicated, may hold values from 0.5 to 1.5
- norm2_gain: float32 [1536], replicated, may hold values from 0.5 to 1.5
- w_query: bfloat16 [1536, 1536], P(None, 'ep')
- key_weight: bfloat16 [1536, 512], P(None, 'ep')
- value_weight: bfloat16 [1536, 512], P(None, 'ep'), may hold values from -0.15625 to 0.15625
- w_out_attn: bfloat16 [1536, 1536], P('ep'), may hold values from -0.15625 to 0.15625
- w_in: bfloat16 [40, 1536, 1024], P('ep'), may hold values from -0.15625 to 0.15625
- w_out: bfloat16 [40, 512, 1536], P('ep'), may hold values from -0.25 to 0.25
- paged_key_value_cache: bfloat16 [96, 8, 2, 64, 64], P('req', 'ep'), may hold values from -6 to 6
- page_table: int32 [64], replicated, may hold values from 0 to 95, as said below
Outputs:
- attn_out: bfloat16 [4096, 1536], P(('req', 'ep'))
- moe_out: bfloat16 [4096, 1536], P(('req', 'ep'))
- new_cache: bfloat16 [96, 8, 2, 64, 64], P('req', 'ep')
Inputs may be any that keep to these rules, and one draw needn't show every extreme that they name: `seg_ids`: segment ids never fall along the stream; the longest prompt holds exactly half of the 4096 tokens. `routes`: each token names 8 different experts; within the rows of one device no expert is named more than 48 times, a bound that some block reaches. `page_table`: entries are distinct.
All inputs are finite; a program needn't handle non-finite values.
Results may differ from a plain program's by a relative error of at most 0.017.
Values may be sent and summed in bfloat16 or wider, within the bound.
No kernel may reach another device: no remote copies, remote signals or barrier semaphores. Data moves between devices by JAX's collectives and lax.ppermute only.
A program may use at most 192 MiB of HBM per device.

v0:
```python
import jax
import jax.numpy as jnp
from jax import lax
from jax.sharding import PartitionSpec as P
from jax.experimental import pallas as pl
from jax.experimental.pallas import tpu as pltpu

HEAD_SIZE = 64
E = 40
PAGE_TOKENS = 64
CAP = 48


norm_eps = 1e-06
score_scale = 0.015625
residual_scale = 0.22
rope_base = 10000.0
neg_fill = -1e30


def rms_scale(rows, gain):
    mean_sq = jnp.mean(rows * rows, axis=-1, keepdims=True)
    return rows * lax.rsqrt(mean_sq + norm_eps) * gain


def positions_of(segments):
    tok_index = jnp.arange(segments.shape[0], dtype=jnp.int32)
    previous = jnp.concatenate([jnp.full((1,), -1, jnp.int32), segments[:-1]])
    starts = jnp.where(segments != previous, tok_index, 0)
    return tok_index - lax.cummax(starts, axis=0)


def rotary_apply(heads_in, token_positions):
    half_dim = heads_in.shape[-1] // 2
    inverse_freq = rope_base ** (
        -jnp.arange(half_dim, dtype=jnp.float32) * 2.0 / heads_in.shape[-1]
    )
    angles = token_positions.astype(jnp.float32)[:, None] * inverse_freq[None, :]
    cos_part = jnp.cos(angles)[:, None, :]
    sine_part = jnp.sin(angles)[:, None, :]
    first_half = heads_in[..., :half_dim]
    second_half = heads_in[..., half_dim:]
    return jnp.concatenate(
        [
            first_half * cos_part - second_half * sine_part,
            second_half * cos_part + first_half * sine_part,
        ],
        axis=-1,
    )


def gather_rows(x, axis_name, axis=0):
    count = lax.axis_size(axis_name)
    spread = jnp.broadcast_to(x[None], (count,) + x.shape)
    got = lax.all_to_all(spread, axis_name, 0, 0, tiled=True)
    got = jnp.moveaxis(got, 0, axis)
    shape = list(x.shape)
    shape[axis] = shape[axis] * count
    return got.reshape(shape)


def scatter_sum_rows(x, axis_name):
    count = lax.axis_size(axis_name)
    parts = x.reshape((count, x.shape[0] // count) + x.shape[1:])
    got = lax.all_to_all(parts, axis_name, 0, 0, tiled=True)
    return jnp.sum(got.astype(jnp.float32), axis=0)


def chip_pairs(count, shift):
    chips = count // 2
    return [(d, ((d // 2 + shift) % chips) * 2 + d % 2) for d in range(count)]


def gather_ep(x):
    count = lax.axis_size("ep")
    if count % 2:
        return gather_rows(x, "ep")
    chips = count // 2
    me = lax.axis_index("ep")
    chip = me // 2
    core = me % 2
    side = [x]
    for shift in range(1, chips):
        side.append(lax.ppermute(x, "ep", chip_pairs(count, shift)))
    side = jnp.stack(side)
    other = lax.ppermute(side, "ep", [(d, d ^ 1) for d in range(count)])
    both = jnp.where(core == 0, jnp.stack([side, other], 1), jnp.stack([other, side], 1))
    order = (chip - jnp.arange(chips, dtype=jnp.int32)) % chips
    full = jnp.take(both, order, axis=0, mode="clip")
    return full.reshape((count * x.shape[0],) + x.shape[1:])


def scatter_sum_ep(p):
    count = lax.axis_size("ep")
    if count % 2:
        return scatter_sum_rows(p, "ep")
    chips = count // 2
    me = lax.axis_index("ep")
    chip = me // 2
    core = me % 2
    rows = p.shape[0] // count
    parts = p.reshape((chips, 2, rows) + p.shape[1:])
    mine = jnp.where(core == 0, parts[:, 0], parts[:, 1])
    theirs = jnp.where(core == 0, parts[:, 1], parts[:, 0])
    got = lax.ppermute(theirs, "ep", [(d, d ^ 1) for d in range(count)])
    sums = mine.astype(jnp.float32) + got.astype(jnp.float32)
    total = lax.dynamic_index_in_dim(sums, chip, 0, keepdims=False)
    for shift in range(1, chips):
        piece = lax.dynamic_index_in_dim(sums, (chip + shift) % chips, 0, keepdims=False)
        total = total + lax.ppermute(
            piece.astype(jnp.bfloat16), "ep", chip_pairs(count, shift)
        ).astype(jnp.float32)
    return total


Q_TILE = 128
K_TILE = 256


def flash_body(lo_ref, hi_ref, q_ref, k_ref, v_ref, tok_ref, begin_ref, o_ref):
    qb = pl.program_id(1)
    ratio = q_ref.shape[1]
    q_tile = q_ref.shape[2]
    head_dim = q_ref.shape[3]
    q = q_ref[0].reshape(ratio * q_tile, head_dim)
    tok = tok_ref[...]
    begin = begin_ref[...]

    def step(kb, carry):
        m_old, l_old, acc_old = carry
        k0 = pl.multiple_of(kb * K_TILE, K_TILE)
        k_blk = k_ref[0, pl.ds(k0, K_TILE), :]
        v_blk = v_ref[0, pl.ds(k0, K_TILE), :]
        s = lax.dot_general(
            q, k_blk, (((1,), (1,)), ((), ())), preferred_element_type=jnp.float32
        )
        s = (s * score_scale).reshape(ratio, q_tile, K_TILE)
        key_at = k0 + lax.broadcasted_iota(jnp.int32, (q_tile, K_TILE), 1)
        allowed = (key_at >= begin) & (key_at <= tok)
        s = jnp.where(allowed[None], s, -jnp.inf)
        m_new = jnp.maximum(m_old, jnp.max(s, axis=-1, keepdims=True))
        alpha = jnp.exp(m_old - m_new)
        p = jnp.exp(s - m_new)
        l_new = alpha * l_old + jnp.sum(p, axis=-1, keepdims=True)
        pv = lax.dot_general(
            p.reshape(ratio * q_tile, K_TILE).astype(jnp.bfloat16),
            v_blk,
            (((1,), (0,)), ((), ())),
            preferred_element_type=jnp.float32,
        )
        acc_new = alpha * acc_old + pv.reshape(ratio, q_tile, head_dim)
        return m_new, l_new, acc_new

    init = (
        jnp.full((ratio, q_tile, 1), neg_fill, jnp.float32),
        jnp.zeros((ratio, q_tile, 1), jnp.float32),
        jnp.zeros((ratio, q_tile, head_dim), jnp.float32),
    )
    m_fin, l_fin, acc_fin = lax.fori_loop(lo_ref[qb], hi_ref[qb] + 1, step, init)
    o_ref[0] = (acc_fin / l_fin).astype(o_ref.dtype)


def flash_attention(query_grouped, kv_all, q_index, q_begin):
    kv_heads, ratio, group_len, head_dim = query_grouped.shape
    n_rows = kv_all.shape[1]
    n_q = group_len // Q_TILE
    lo = jnp.min(q_begin.reshape(n_q, Q_TILE), axis=1) // K_TILE
    hi = jnp.max(q_index.reshape(n_q, Q_TILE), axis=1) // K_TILE
    grid_spec = pltpu.PrefetchScalarGridSpec(
        num_scalar_prefetch=2,
        grid=(kv_heads, n_q),
        in_specs=[
            pl.BlockSpec((1, ratio, Q_TILE, head_dim), lambda g, qb, lo, hi: (g, 0, qb, 0)),
            pl.BlockSpec((1, n_rows, head_dim), lambda g, qb, lo, hi: (g, 0, 0)),
            pl.BlockSpec((1, n_rows, head_dim), lambda g, qb, lo, hi: (kv_heads + g, 0, 0)),
            pl.BlockSpec((Q_TILE, 1), lambda g, qb, lo, hi: (qb, 0)),
            pl.BlockSpec((Q_TILE, 1), lambda g, qb, lo, hi: (qb, 0)),
        ],
        out_specs=pl.BlockSpec((1, ratio, Q_TILE, head_dim), lambda g, qb, lo, hi: (g, 0, qb, 0)),
    )
    out = pl.pallas_call(
        flash_body,
        grid_spec=grid_spec,
        out_shape=jax.ShapeDtypeStruct(query_grouped.shape, jnp.bfloat16),
    )(lo, hi, query_grouped, kv_all, kv_all, q_index[:, None], q_begin[:, None])
    return out


def body(
    tokens,
    seg_ids,
    routes,
    route_weights,
    norm1_gain,
    norm2_gain,
    w_query,
    key_weight,
    value_weight,
    w_out_attn,
    w_in,
    w_out,
    paged_key_value_cache,
    page_table,
):
    tok_dev = tokens.shape[0]
    ep_count = lax.axis_size("ep")
    group_len = tok_dev * ep_count
    req_pos = lax.axis_index("req")
    all_segs = gather_rows(seg_ids, ("req", "ep"))
    all_pos = positions_of(all_segs)
    group_start = req_pos * group_len
    group_pos = lax.dynamic_slice_in_dim(all_pos, group_start, group_len)
    group_seg = lax.dynamic_slice_in_dim(all_segs, group_start, group_len)
    normed = rms_scale(tokens.astype(jnp.float32), norm1_gain).astype(jnp.bfloat16)
    joined = jnp.concatenate([w_query, key_weight, value_weight], axis=1)
    projected = jnp.dot(
        gather_ep(normed), joined, preferred_element_type=jnp.float32
    )
    query_width = w_query.shape[1]
    kv_width = key_weight.shape[1]
    q_heads = query_width // HEAD_SIZE
    kv_heads = kv_width // HEAD_SIZE
    heads_ratio = q_heads // kv_heads
    query_rows = rotary_apply(
        projected[:, :query_width].reshape(group_len, q_heads, HEAD_SIZE), group_pos
    ).astype(jnp.bfloat16)
    key_rows = rotary_apply(
        projected[:, query_width : query_width + kv_width].reshape(
            group_len, kv_heads, HEAD_SIZE
        ),
        group_pos,
    ).astype(jnp.bfloat16)
    value_rows = (
        projected[:, query_width + kv_width :]
        .astype(jnp.bfloat16)
        .reshape(group_len, kv_heads, HEAD_SIZE)
    )
    query_grouped = query_rows.reshape(group_len, kv_heads, heads_ratio, HEAD_SIZE).transpose(
        1, 2, 0, 3
    )
    kv_local = jnp.concatenate(
        [key_rows.transpose(1, 0, 2), value_rows.transpose(1, 0, 2)], axis=0
    )
    kv_all = gather_rows(kv_local, "req", axis=1)
    n_rows = kv_all.shape[1]
    q_index = group_start + jnp.arange(group_len, dtype=jnp.int32)
    q_begin = q_index - group_pos
    head_out = flash_attention(query_grouped, kv_all, q_index, q_begin)
    pages_here = paged_key_value_cache.shape[0]
    page_first = req_pos * pages_here
    piece_pages = n_rows // PAGE_TOKENS
    local_pages = page_first + jnp.arange(pages_here, dtype=jnp.int32)
    match = local_pages[:, None] == page_table[None, :]
    hit = jnp.any(match, axis=1)
    block_of = jnp.argmax(match, axis=1).astype(jnp.int32)
    kv_paged = kv_all.reshape(2, kv_heads, piece_pages, PAGE_TOKENS, HEAD_SIZE)
    picked = jnp.take(kv_paged, block_of, axis=2, mode="clip").transpose(2, 1, 0, 3, 4)
    new_cache = jnp.where(hit[:, None, None, None, None], picked, paged_key_value_cache)
    head_out = head_out.transpose(2, 0, 1, 3).reshape(group_len, query_width)
    attention = scatter_sum_ep(
        jnp.dot(head_out, w_out_attn, preferred_element_type=jnp.float32).astype(jnp.bfloat16)
    )
    attn_out = attention.astype(jnp.bfloat16)
    moe_in = rms_scale(tokens.astype(jnp.float32) + residual_scale * attention, norm2_gain).astype(
        jnp.bfloat16
    )
    ffe_width = w_out.shape[1]
    exp_here = w_in.shape[0]
    expert_ids = jnp.arange(E, dtype=jnp.int32)
    shares = jnp.sum(
        jnp.where(routes[:, :, None] == expert_ids[None, None, :], route_weights[:, :, None], 0.0),
        axis=1,
    )
    rows_all = gather_ep(moe_in)
    shares_all = gather_rows(shares, "ep")
    first_expert = lax.axis_index("ep") * exp_here
    shares_here = lax.dynamic_slice_in_dim(shares_all, first_expert, exp_here, 1)
    total_rows = rows_all.shape[0]
    chosen = (shares_here > 0.0).astype(jnp.int32).reshape(ep_count, tok_dev, exp_here)
    slot_in = jnp.cumsum(chosen, axis=1) - 1
    source_ids = jnp.arange(ep_count, dtype=jnp.int32)[:, None, None]
    local_slot = (source_ids * CAP + slot_in).reshape(total_rows, exp_here)
    live = (chosen > 0).reshape(total_rows, exp_here)
    slot_ids = jnp.arange(ep_count * CAP, dtype=jnp.int32)
    dispatch = (local_slot.T[:, None, :] == slot_ids[None, :, None]) & live.T[:, None, :]
    arrived = jnp.einsum(
        "esr,rd->esd", dispatch.astype(jnp.bfloat16), rows_all, preferred_element_type=jnp.float32
    ).astype(jnp.bfloat16)
    gate_up = jnp.einsum("esd,edf->esf", arrived, w_in, preferred_element_type=jnp.float32)
    activated = (jax.nn.silu(gate_up[..., :ffe_width]) * gate_up[..., ffe_width:]).astype(
        jnp.bfloat16
    )
    result = jnp.einsum(
        "esf,efd->esd", activated, w_out, preferred_element_type=jnp.float32
    ).astype(jnp.bfloat16)
    combine = jnp.where(dispatch, shares_here.T[:, None, :], 0.0)
    combine_hi = combine.astype(jnp.bfloat16)
    combine_lo = (combine - combine_hi.astype(jnp.float32)).astype(jnp.bfloat16)
    partial_rows = jnp.einsum(
        "esr,esd->rd", combine_hi, result, preferred_element_type=jnp.float32
    ) + jnp.einsum("esr,esd->rd", combine_lo, result, preferred_element_type=jnp.float32)
    moe_out = scatter_sum_ep(partial_rows.astype(jnp.bfloat16)).astype(jnp.bfloat16)
    return (attn_out, moe_out, new_cache)


def solution(mesh):
    in_specs = (
        P(("req", "ep"), None),
        P(("req", "ep")),
        P(("req", "ep"), None),
        P(("req", "ep"), None),
        P(),
        P(),
        P(None, "ep"),
        P(None, "ep"),
        P(None, "ep"),
        P("ep", None),
        P("ep", None, None),
        P("ep", None, None),
        P("req", "ep", None, None, None),
        P(),
    )
    out_specs = (P(("req", "ep"), None), P(("req", "ep"), None), P("req", "ep", None, None, None))
    return jax.shard_map(body, mesh=mesh, in_specs=in_specs, out_specs=out_specs, check_vma=False)
```

profile of v0, /device:TPU:12, one launch (start us, length us, event | category | flops | bytes accessed | tf_op | source)
XLA Modules:
  0.0 216.4 jit_solution(6660260392032588435)
XLA Ops:
  2.0 6.0 %all-to-all-start = ((s32[32,1,128]{2,1,0:T(1,128)}), s32[32,1,128]{2,1,0:T(1,128)S(1)}, u32[]{:S(2)}, u32[]{:S(2)}) async-start(s32[32,1,128]{2,1,0:T(1,128)} %broadcast_in_dim.43), calls=%async_computation | async-start | bytes 32768 | tf_op jit(solution)/shard_map/all_to_all | solution.py:55
  10.3 1.5 collective-permute-start
  14.2 7.4 %collective-permute-done = bf16[128,1536]{1,0:T(8,128)(2,1)S(1)} collective-permute-done((bf16[128,1536]{1,0:T(8,128)(2,1)S(1)}, bf16[128,1536]{1,0:T(8,128)(2,1)S(1)}, u32[]{:S(2)}, u32[]{:S(2)}) %collective-permute-start) | collective-permute-done | bytes 393248 | tf_op jit(solution)/shard_map/ppermute | solution.py:84
  26.5 1.6 multiply_cosine_fusion
  29.0 1.6 maximum_select_fusion
  30.6 2.1 gather_fusion
  32.7 3.3 %fusion.15 = f32[512,640]{1,0:T(8,128)S(1)} fusion(bf16[512,1536]{1,0:T(8,128)(2,1)} %bitcast.146, bf16[1536,128]{1,0:T(8,128)(2,1)S(1)} %copy-done.17, bf16[1536,128]{1,0:T(8,128)(2,1)} %param.21, bf16[1536,384]{1,0:T(8,128)(2,1)} %param.20), kind=kOutput, calls=%fused_computation.19 | convolution fusion | flops 1012531200 | bytes 4849664 | tf_op jit(solution)/shard_map/dot_general | solution.py:216
  37.4 1.6 broadcast_in_dim.49
  39.0 6.1 %all-to-all-start.1 = ((bf16[8,4,512,64]{2,3,1,0:T(8,128)(2,1)}), bf16[8,4,512,64]{2,3,1,0:T(8,128)(2,1)S(1)}, u32[]{:S(2)}, u32[]{:S(2)}) async-start(bf16[8,4,512,64]{2,3,1,0:T(8,128)(2,1)} %broadcast_in_dim.49), calls=%async_computation.1 | async-start | bytes 4194304 | tf_op jit(solution)/shard_map/all_to_all | solution.py:55
  48.3 2.1 slice.79
  50.3 2.3 %copy.88 = f32[512,384]{0,1:T(8,128)} copy(f32[512,384]{1,0:T(8,128)} %slice.79) | data formatting | bytes 1572864 | tf_op jit(solution)/shard_map/slice | solution.py:225
  52.6 1.9 subtract_convert_fusion
  54.5 2.1 copy.89
  57.8 2.7 %maximum_bitcast_fusion.q_ref = bf16[2,3,512,64]{3,2,1,0:T(8,128)(2,1)} fusion(bf16[512,2,3,32]{3,0,2,1:T(8,128)(2,1)} %bitcast.142, bf16[512,2,3,32]{3,0,2,1:T(8,128)(2,1)} %bitcast.141), kind=kLoop, calls=%fused_computation.51 | loop fusion | flops 786432 | bytes 786432 | tf_op jit(solution)/shard_map/transpose | solution.py:238
  60.5 30.2 %all-to-all-done.1 = bf16[8,4,512,64]{2,3,1,0:T(8,128)(2,1)S(1)} async-done(((bf16[8,4,512,64]{2,3,1,0:T(8,128)(2,1)}), bf16[8,4,512,64]{2,3,1,0:T(8,128)(2,1)S(1)}, u32[]{:S(2)}, u32[]{:S(2)}) %all-to-all-start.1) | async-done | bytes 2097184 | tf_op jit(solution)/shard_map/all_to_all | solution.py:55
  90.7 3.1 %copy.93 = bf16[4,8,512,64]{3,2,1,0:T(8,128)(2,1)} copy(bf16[4,8,512,64]{2,3,0,1:T(8,128)(2,1)S(1)} %bitcast.137) | data formatting | bytes 4194304 | tf_op jit(solution)/shard_map/transpose | solution.py:56
  93.8 30.1 %shard_map.157 = bf16[2,3,512,64]{3,2,1,0:T(8,128)(2,1)} custom-call(s32[4]{0:T(128)} %get-tuple-element.34.lo_ref, s32[4]{0:T(128)} %get-tuple-element.33.hi_ref, bf16[2,3,512,64]{3,2,1,0:T(8,128)(2,1)} %maximum_bitcast_fusion.q_ref, bf16[4,4096,64]{2,1,0:T(8,128)(2,1)} %bitcast.132, bf16[4,4096,64]{2,1,0:T(8,128)(2,1)} %bitcast.133, ...), custom_call_target="tpu_custom_call" | custom-call | tf_op jit(solution)/shard_map/pallas_call | solution.py:181
  126.6 2.2 %collective-permute-done.2 = bf16[2,128,1536]{2,1,0:T(8,128)(2,1)S(1)} collective-permute-done((bf16[2,128,1536]{2,1,0:T(8,128)(2,1)S(1)}, bf16[2,128,1536]{2,1,0:T(8,128)(2,1)S(1)}, u32[]{:S(2)}, u32[]{:S(2)}) %collective-permute-start.2) | collective-permute-done | bytes 786464 | tf_op jit(solution)/shard_map/ppermute | solution.py:105
  130.3 1.5 collective-permute-start.3
  131.9 9.7 %collective-permute-done.3 = bf16[128,1536]{1,0:T(8,128)(2,1)S(1)} collective-permute-done((bf16[128,1536]{1,0:T(8,128)(2,1)S(1)}, bf16[128,1536]{1,0:T(8,128)(2,1)S(1)}, u32[]{:S(2)}, u32[]{:S(2)}) %collective-permute-start.3) | collective-permute-done | bytes 393248 | tf_op jit(solution)/shard_map/ppermute | solution.py:110
  141.5 1.4 multiply_reduce_fusion
  143.9 1.5 collective-permute-start.4
  146.1 3.5 %all-to-all-start.2 = ((f32[4,128,40]{1,2,0:T(8,128)}), f32[4,128,40]{1,2,0:T(8,128)S(1)}, u32[]{:S(2)}, u32[]{:S(2)}) async-start(f32[4,128,40]{1,2,0:T(8,128)} %broadcast_in_dim.53), calls=%async_computation.2 | async-start | bytes 163840 | tf_op jit(solution)/shard_map/all_to_all | solution.py:55
  149.6 5.0 %collective-permute-done.4 = bf16[128,1536]{1,0:T(8,128)(2,1)S(1)} collective-permute-done((bf16[128,1536]{1,0:T(8,128)(2,1)S(1)}, bf16[128,1536]{1,0:T(8,128)(2,1)S(1)}, u32[]{:S(2)}, u32[]{:S(2)}) %collective-permute-start.4) | collective-permute-done | bytes 393248 | tf_op jit(solution)/shard_map/ppermute | solution.py:84
  157.4 2.0 gather_fusion.1
  159.4 17.3 %fusion = f32[10,192,1024]{2,1,0:T(8,128)} fusion(bf16[10,1536,1024]{2,1,0:T(8,128)(2,1)} %param.24, bf16[512,1536,1]{1,0,2:T(8,128)(2,1)} %bitcast.145, s32[10,512]{1,0:T(8,128)S(1)} %copy.100, pred[10,512]{1,0:T(8,128)(4,1)S(1)} %get-tuple-element.17), kind=kOutput, calls=%fused_computation.3 | convolution fusion | flops 9064611840 | bytes 40920064 | tf_op jit(solution)/shard_map/esd,edf->esf/dot_general | solution.py:289
  176.7 13.6 %convolution_convert_fusion = bf16[10,192,1536]{2,1,0:T(8,128)(2,1)} fusion(bf16[10,512,1536]{2,1,0:T(8,128)(2,1)} %param.25, f32[10,192,1024]{2,1,0:T(8,128)} %fusion), kind=kOutput, calls=%fused_computation.7 | convolution fusion | flops 3028746240 | bytes 29491200 | tf_op jit(solution)/shard_map/esf,efd->esd/dot_general | solution.py:293
  190.3 6.3 %convolution_bitcast_fusion = f32[512,1536]{1,0:T(8,128)S(1)} fusion(bf16[10,192,1536]{2,1,0:T(8,128)(2,1)} %convolution_convert_fusion, f32[10,512]{1,0:T(8,128)S(1)} %dynamic-slice_bitcast_fusion, s32[10,512]{1,0:T(8,128)S(1)} %copy.100, pred[10,512]{1,0:T(8,128)(4,1)S(1)} %get-tuple-element.17), kind=kOutput, calls=%fused_computation.14 | convolution fusion | flops 3026780160 | bytes 9090048 | tf_op jit(solution)/shard_map/esr,esd->rd/dot_general | solution.py:301
  196.6 3.8 %fusion.12 = bf16[512,1536]{1,0:T(8,128)(2,1)S(1)} fusion(f32[512,1536]{1,0:T(8,128)S(1)} %convolution_bitcast_fusion, bf16[10,192,1536]{2,1,0:T(8,128)(2,1)S(1)} %copy-done.18, f32[10,512]{1,0:T(8,128)S(1)} %dynamic-slice_bitcast_fusion, s32[10,512]{1,0:T(8,128)S(1)} %copy.100, pred[10,512]{1,0:T(8,128)(4,1)S(1)} %get-tuple-element.17), kind=kOutput, calls=%fused_computation.18 | convolution fusion | flops 3024420864 | bytes 10662912 | tf_op jit(solution)/shard_map/esr,esd->rd/dot_general | solution.py:299
  204.4 1.5 collective-permute-start.7
  205.9 2.9 %gather_fusion.2 = bf16[12,2,2,64,64]{4,3,2,1,0:T(8,128)(2,1)S(1)} fusion(bf16[2,2,64,64,64]{4,3,2,1,0:T(8,128)(2,1)} %bitcast.134, s32[1024]{0:T(1024)S(1)} %pad_clamp_fusion), kind=kCustom, calls=%fused_computation.2 | custom fusion | bytes 786480 | tf_op jit(solution)/shard_map/jit(_take)/gather | solution.py:257
  209.9 5.7 %collective-permute-done.7 = bf16[128,1536]{1,0:T(8,128)(2,1)S(1)} collective-permute-done((bf16[128,1536]{1,0:T(8,128)(2,1)S(1)}, bf16[128,1536]{1,0:T(8,128)(2,1)S(1)}, u32[]{:S(2)}, u32[]{:S(2)}) %collective-permute-start.7) | collective-permute-done | bytes 393248 | tf_op jit(solution)/shard_map/ppermute | solution.py:110
  (107 shorter events, 31.8 us)
Async XLA Ops:
  0.6 124.7 %copy-start = (bf16[384,1536]{1,0:T(8,128)(2,1)S(1)}, bf16[384,1536]{1,0:T(8,128)(2,1)}, u32[]{:S(2)}) copy-start(bf16[384,1536]{1,0:T(8,128)(2,1)} %param.23) | copy-start | bytes 3538948
  2.0 19.8 %all-to-all-start = ((s32[32,1,128]{2,1,0:T(1,128)}), s32[32,1,128]{2,1,0:T(1,128)S(1)}, u32[]{:S(2)}, u32[]{:S(2)}) async-start(s32[32,1,128]{2,1,0:T(1,128)} %broadcast_in_dim.43), calls=%async_computation | async-start | bytes 32768 | tf_op jit(solution)/shard_map/all_to_all | solution.py:55
  10.3 11.2 %collective-permute-start = (bf16[128,1536]{1,0:T(8,128)(2,1)S(1)}, bf16[128,1536]{1,0:T(8,128)(2,1)S(1)}, u32[]{:S(2)}, u32[]{:S(2)}) collective-permute-start(bf16[128,1536]{1,0:T(8,128)(2,1)S(1)} %fusion.36), channel_id=1, source_target_pairs={{0,2},{1,3},{2,0},{3,1},{4,6},{5,7},{6,4},{7,5},{8,10},{9,11},{10,... | collective-permute-start | bytes 1179656 | tf_op jit(solution)/shard_map/ppermute | solution.py:84
  21.7 6.4 %collective-permute-start.1 = (bf16[2,128,1536]{2,1,0:T(8,128)(2,1)S(1)}, bf16[2,128,1536]{2,1,0:T(8,128)(2,1)S(1)}, u32[]{:S(2)}, u32[]{:S(2)}) collective-permute-start(bf16[2,128,1536]{2,1,0:T(8,128)(2,1)S(1)} %get-tuple-element.28), channel_id=1, source_target_pairs={{0,1},{1,0},{2,3},{3,2},{4,5},{5,4},{6,7},{7,6},{8,9},{9,8},{10,11... | collective-permute-start | bytes 2359304 | tf_op jit(solution)/shard_map/ppermute | solution.py:86
  26.4 1.7 copy-start.12
  28.1 0.9 copy-start.9
  30.6 2.1 copy-start.17
  32.7 4.6 %copy-start.10 = (f32[512,32]{0,1:T(8,128)S(1)}, f32[512,32]{0,1:T(8,128)}, u32[]{:S(2)}) copy-start(f32[512,32]{0,1:T(8,128)} %get-tuple-element.31) | copy-start | bytes 196612
  32.7 4.6 %copy-start.11 = (f32[512,32]{0,1:T(8,128)S(1)}, f32[512,32]{0,1:T(8,128)}, u32[]{:S(2)}) copy-start(f32[512,32]{0,1:T(8,128)} %get-tuple-element.32) | copy-start | bytes 196612
  36.0 1.1 copy-start.7
  39.0 51.7 %all-to-all-start.1 = ((bf16[8,4,512,64]{2,3,1,0:T(8,128)(2,1)}), bf16[8,4,512,64]{2,3,1,0:T(8,128)(2,1)S(1)}, u32[]{:S(2)}, u32[]{:S(2)}) async-start(bf16[8,4,512,64]{2,3,1,0:T(8,128)(2,1)} %broadcast_in_dim.49), calls=%async_computation.1 | async-start | bytes 4194304 | tf_op jit(solution)/shard_map/all_to_all | solution.py:55
  126.5 2.4 %collective-permute-start.2 = (bf16[2,128,1536]{2,1,0:T(8,128)(2,1)S(1)}, bf16[2,128,1536]{2,1,0:T(8,128)(2,1)S(1)}, u32[]{:S(2)}, u32[]{:S(2)}) collective-permute-start(bf16[2,128,1536]{2,1,0:T(8,128)(2,1)S(1)} %select_bitcast_fusion.1), channel_id=1, source_target_pairs={{0,1},{1,0},{2,3},{3,2},{4,5},{5,4},{6,7},{7,6},{8,9},{9,8},{10,11... | collective-permute-start | bytes 2359304 | tf_op jit(solution)/shard_map/ppermute | solution.py:105
  126.6 15.0 %copy-start.2 = (bf16[128,1536]{1,0:T(8,128)(2,1)S(1)}, bf16[128,1536]{1,0:T(8,128)(2,1)}, u32[]{:S(2)}) copy-start(bf16[128,1536]{1,0:T(8,128)(2,1)} %param.14) | copy-start | bytes 1179652
  129.1 1.2 copy-start.3
  130.3 12.7 %copy-start.13 = (f32[1536]{0:T(1024)S(1)}, f32[1536]{0:T(1024)}, u32[]{:S(2)}) copy-start(f32[1536]{0:T(1024)} %param.19) | copy-start | bytes 18436
  130.3 12.6 %copy-start.4 = (f32[2,128,1536]{2,1,0:T(8,128)S(1)}, f32[2,128,1536]{2,1,0:T(8,128)}, u32[]{:S(2)}) copy-start(f32[2,128,1536]{2,1,0:T(8,128)} %copy-done.3) | copy-start | bytes 4718596
  130.3 11.2 %collective-permute-start.3 = (bf16[128,1536]{1,0:T(8,128)(2,1)S(1)}, bf16[128,1536]{1,0:T(8,128)(2,1)S(1)}, u32[]{:S(2)}, u32[]{:S(2)}) collective-permute-start(bf16[128,1536]{1,0:T(8,128)(2,1)S(1)} %fusion.38), channel_id=1, source_target_pairs={{0,2},{1,3},{2,0},{3,1},{4,6},{5,7},{6,4},{7,5},{8,10},{9,11},{10,... | collective-permute-start | bytes 1179656 | tf_op jit(solution)/shard_map/ppermute | solution.py:110
  131.9 13.5 %copy-start.14 = (f32[128,8]{0,1:T(8,128)S(1)}, f32[128,8]{0,1:T(8,128)}, u32[]{:S(2)}) copy-start(f32[128,8]{0,1:T(8,128)} %param.17) | copy-start | bytes 12292
  131.9 13.5 %copy-start.15 = (s32[128,8]{0,1:T(8,128)S(1)}, s32[128,8]{0,1:T(8,128)}, u32[]{:S(2)}) copy-start(s32[128,8]{0,1:T(8,128)} %param.16) | copy-start | bytes 12292
  143.9 10.8 %collective-permute-start.4 = (bf16[128,1536]{1,0:T(8,128)(2,1)S(1)}, bf16[128,1536]{1,0:T(8,128)(2,1)S(1)}, u32[]{:S(2)}, u32[]{:S(2)}) collective-permute-start(bf16[128,1536]{1,0:T(8,128)(2,1)S(1)} %get-tuple-element.21), channel_id=1, source_target_pairs={{0,2},{1,3},{2,0},{3,1},{4,6},{5,7},{6,4},{7,5},{8,10},{9,11},{10,... | collective-permute-start | bytes 1179656 | tf_op jit(solution)/shard_map/ppermute | solution.py:84
  146.1 9.1 %all-to-all-start.2 = ((f32[4,128,40]{1,2,0:T(8,128)}), f32[4,128,40]{1,2,0:T(8,128)S(1)}, u32[]{:S(2)}, u32[]{:S(2)}) async-start(f32[4,128,40]{1,2,0:T(8,128)} %broadcast_in_dim.53), calls=%async_computation.2 | async-start | bytes 163840 | tf_op jit(solution)/shard_map/all_to_all | solution.py:55
  154.8 2.4 %collective-permute-start.5 = (bf16[2,128,1536]{2,1,0:T(8,128)(2,1)S(1)}, bf16[2,128,1536]{2,1,0:T(8,128)(2,1)S(1)}, u32[]{:S(2)}, u32[]{:S(2)}) collective-permute-start(bf16[2,128,1536]{2,1,0:T(8,128)(2,1)S(1)} %get-tuple-element.26), channel_id=1, source_target_pairs={{0,1},{1,0},{2,3},{3,2},{4,5},{5,4},{6,7},{7,6},{8,9},{9,8},{10,11... | collective-permute-start | bytes 2359304 | tf_op jit(solution)/shard_map/ppermute | solution.py:86
  190.3 6.3 %copy-start.18 = (bf16[10,192,1536]{2,1,0:T(8,128)(2,1)S(1)}, bf16[10,192,1536]{2,1,0:T(8,128)(2,1)}, u32[]{:S(2)}) copy-start(bf16[10,192,1536]{2,1,0:T(8,128)(2,1)} %convolution_convert_fusion) | copy-start | bytes 17694724
  200.4 0.7 copy-start.16
  200.5 2.4 %collective-permute-start.6 = (bf16[2,128,1536]{2,1,0:T(8,128)(2,1)S(1)}, bf16[2,128,1536]{2,1,0:T(8,128)(2,1)S(1)}, u32[]{:S(2)}, u32[]{:S(2)}) collective-permute-start(bf16[2,128,1536]{2,1,0:T(8,128)(2,1)S(1)} %select_bitcast_fusion), channel_id=1, source_target_pairs={{0,1},{1,0},{2,3},{3,2},{4,5},{5,4},{6,7},{7,6},{8,9},{9,8},{10,11... | collective-permute-start | bytes 2359304 | tf_op jit(solution)/shard_map/ppermute | solution.py:105
  203.2 1.2 copy-start.5
  204.3 4.5 %copy-start.8 = (bf16[12,2,2,64,64]{4,3,2,1,0:T(8,128)(2,1)S(1)}, bf16[12,2,2,64,64]{4,3,2,1,0:T(8,128)(2,1)}, u32[]{:S(2)}) copy-start(bf16[12,2,2,64,64]{4,3,2,1,0:T(8,128)(2,1)} %param.26) | copy-start | bytes 1179652
  204.4 11.2 %collective-permute-start.7 = (bf16[128,1536]{1,0:T(8,128)(2,1)S(1)}, bf16[128,1536]{1,0:T(8,128)(2,1)S(1)}, u32[]{:S(2)}, u32[]{:S(2)}) collective-permute-start(bf16[128,1536]{1,0:T(8,128)(2,1)S(1)} %fusion.39), channel_id=1, source_target_pairs={{0,2},{1,3},{2,0},{3,1},{4,6},{5,7},{6,4},{7,5},{8,10},{9,11},{10,... | collective-permute-start | bytes 1179656 | tf_op jit(solution)/shard_map/ppermute | solution.py:110
  208.8 6.8 %copy-start.6 = (f32[2,128,1536]{2,1,0:T(8,128)S(1)}, f32[2,128,1536]{2,1,0:T(8,128)}, u32[]{:S(2)}) copy-start(f32[2,128,1536]{2,1,0:T(8,128)} %copy-done.5) | copy-start | bytes 4718596
  208.8 7.6 %copy-start.1 = (bf16[384,1536]{1,0:T(8,128)(2,1)S(1)}, bf16[384,1536]{1,0:T(8,128)(2,1)}, u32[]{:S(2)}) copy-start(bf16[384,1536]{1,0:T(8,128)(2,1)} %param.23) | copy-start | bytes 3538948
where the time goes:
time: 220 us; the launch traced here: 216 us
  waiting for transfers between devices  62.7 us (28%)
  matrix products  45.3 us (21%)
  local copies, waits for them, and re-layouts  31.3 us (14%)
  Pallas kernels  30.1 us (14%)
  other arithmetic  23.9 us (11%)
  starting transfers between devices  22.1 us (10%)
    all_to_all x3, waiting for transfers between devices, gather_rows(): got = lax.all_to_all(spread, axis_name, 0, 0, tiled=True)  30.5 us
    pallas_call x1, Pallas kernels, flash_attention(): pl.pallas_call(flash_body, grid_spec=grid_spec, out_shape=jax.ShapeDtypeS...  30.1 us
    dot_general x1, matrix products, body(): jnp.einsum('esd,edf->esf', arrived, w_in, preferred_element_type=jnp.floa...  17.3 us
    all_to_all x3, starting transfers between devices, gather_rows(): got = lax.all_to_all(spread, axis_name, 0, 0, tiled=True)  15.5 us
    ppermute x2, waiting for transfers between devices, scatter_sum_ep(): lax.ppermute(piece.astype(jnp.bfloat16), 'ep', chip_pairs(count, shift))  15.3 us
    dot_general x1, matrix products, body(): jnp.einsum('esf,efd->esd', activated, w_out, preferred_element_type=jnp.f...  13.6 us
    ppermute x2, waiting for transfers between devices, gather_ep(): side.append(lax.ppermute(x, 'ep', chip_pairs(count, shift)))  12.4 us
    dot_general x1, matrix products, body(): jnp.einsum('esr,esd->rd', combine_lo, result, preferred_element_type=jnp....  6.25 us
  transfers between devices with their start and end apart: 11, of which 9 were waited for; matrix products, arithmetic and copies ran while one was open for 15% of the time, Pallas kernels for 0%

commit v1 on v0

--- a/solution.py
+++ b/solution.py
@@ -294,11 +294,9 @@
         "esf,efd->esd", activated, w_out, preferred_element_type=jnp.float32
     ).astype(jnp.bfloat16)
     combine = jnp.where(dispatch, shares_here.T[:, None, :], 0.0)
-    combine_hi = combine.astype(jnp.bfloat16)
-    combine_lo = (combine - combine_hi.astype(jnp.float32)).astype(jnp.bfloat16)
     partial_rows = jnp.einsum(
-        "esr,esd->rd", combine_hi, result, preferred_element_type=jnp.float32
-    ) + jnp.einsum("esr,esd->rd", combine_lo, result, preferred_element_type=jnp.float32)
+        "esr,esd->rd", combine.astype(jnp.bfloat16), result, preferred_element_type=jnp.float32
+    )
     moe_out = scatter_sum_ep(partial_rows.astype(jnp.bfloat16)).astype(jnp.bfloat16)
     return (attn_out, moe_out, new_cache)
 

time: 220 us -> 212 us (0.964); the launches traced: 216 us -> 211 us
  waiting for transfers between devices: 62.7 us -> 74.3 us
  matrix products: 45.3 us -> 36.1 us
  other arithmetic: 23.9 us -> 17.2 us
  local copies, waits for them, and re-layouts: 31.3 us -> 25.9 us
  Pallas kernels: 30.1 us -> 34.1 us
    dot_general x3 -> x1, matrix products: 23.7 us -> 14.5 us  [body(): jnp.einsum('esr,esd->rd', combine.astype(jnp.bfloat16), result, preferred...]
    all_to_all x3, waiting for transfers between devices: 30.5 us -> 39.4 us  [gather_rows(): got = lax.all_to_all(spread, axis_name, 0, 0, tiled=True)]
    pallas_call x1, Pallas kernels: 30.1 us -> 34.1 us  [flash_attention(): pl.pallas_call(flash_body, grid_spec=grid_spec, out_shape=jax.ShapeDtypeS...]
    another operation x4, other arithmetic: 4.31 us -> 0.5 us
    another operation x3, local copies, waits for them, and re-layouts: 4.06 us -> 0.86 us
    slice x2, local copies, waits for them, and re-layouts: 4.37 us -> 1.45 us  [body(): projected[:, :query_width].reshape(group_len, q_heads, HEAD_SIZE)]
    unnamed x39 -> x29, local copies, waits for them, and re-layouts: 5.56 us -> 5.54 us
  transfers between devices with their start and end apart: 11 -> 11, of which waited for: 9 -> 10; matrix products, arithmetic and copies ran while one was open for 15% -> 8% of each run, Pallas kernels for 0% -> 0%
where the time goes in v1:
time: 212 us; the launch traced here: 211 us
  waiting for transfers between devices  74.3 us (35%)
  matrix products  36.1 us (17%)
  Pallas kernels  34.1 us (16%)
  local copies, waits for them, and re-layouts  25.9 us (12%)
  starting transfers between devices  22 us (10%)
  other arithmetic  17.2 us (8%)
    all_to_all x3, waiting for transfers between devices, gather_rows(): got = lax.all_to_all(spread, axis_name, 0, 0, tiled=True)  39.4 us
    pallas_call x1, Pallas kernels, flash_attention(): pl.pallas_call(flash_body, grid_spec=grid_spec, out_shape=jax.ShapeDtypeS...  34.1 us
    dot_general x1, matrix products, body(): jnp.einsum('esd,edf->esf', arrived, w_in, preferred_element_type=jnp.floa...  17.3 us
    all_to_all x3, starting transfers between devices, gather_rows(): got = lax.all_to_all(spread, axis_name, 0, 0, tiled=True)  15.5 us
    ppermute x2, waiting for transfers between devices, scatter_sum_ep(): lax.ppermute(piece.astype(jnp.bfloat16), 'ep', chip_pairs(count, shift))  15.3 us
    dot_general x1, matrix products, body(): jnp.einsum('esr,esd->rd', combine.astype(jnp.bfloat16), result, preferred...  14.5 us
    ppermute x2, waiting for transfers between devices, gather_ep(): side.append(lax.ppermute(x, 'ep', chip_pairs(count, shift)))  13.8 us
    unnamed x29, local copies, waits for them, and re-layouts  5.54 us
  transfers between devices with their start and end apart: 11, of which 10 were waited for; matrix products, arithmetic and copies ran while one was open for 8% of the time, Pallas kernels for 0%

profile of v1, /device:TPU:12, one launch (start us, length us, event | category | flops | bytes accessed | tf_op | source)
XLA Modules:
  0.0 210.7 jit_solution(15316811365828167967)
XLA Ops:
  0.7 1.4 broadcast_in_dim.43
  2.0 6.0 %all-to-all-start = ((s32[32,1,128]{2,1,0:T(1,128)}), s32[32,1,128]{2,1,0:T(1,128)S(1)}, u32[]{:S(2)}, u32[]{:S(2)}) async-start(s32[32,1,128]{2,1,0:T(1,128)} %broadcast_in_dim.43), calls=%async_computation | async-start | bytes 32768 | tf_op jit(solution)/shard_map/all_to_all | solution.py:55
  9.2 1.2 fusion.40
  10.4 1.5 collective-permute-start
  12.8 8.8 %collective-permute-done = bf16[128,1536]{1,0:T(8,128)(2,1)S(1)} collective-permute-done((bf16[128,1536]{1,0:T(8,128)(2,1)S(1)}, bf16[128,1536]{1,0:T(8,128)(2,1)S(1)}, u32[]{:S(2)}, u32[]{:S(2)}) %collective-permute-start) | collective-permute-done | bytes 393248 | tf_op jit(solution)/shard_map/ppermute | solution.py:84
  23.7 1.2 collective-permute-done.1
  25.8 2.1 %maximum_select_fusion = bf16[2,2,128,1536]{3,2,0,1:T(8,128)(2,1)S(1)} fusion(bf16[2,1,128,1536]{3,2,0,1:T(8,128)(2,1)} %bitcast.144, bf16[2,1,128,1536]{3,2,0,1:T(8,128)(2,1)} %get-tuple-element.27, pred[]{:T(512)S(6)} %eq.32), kind=kLoop, calls=%fused_computation.30 | loop fusion | flops 2359296 | bytes 3145729 | tf_op jit(solution)/shard_map/jit(_where)/select_n | solution.py:87
  27.9 1.8 gather_fusion
  29.7 3.4 %fusion.22 = f32[512,640]{1,0:T(8,128)S(1)} fusion(bf16[512,1536]{1,0:T(8,128)(2,1)} %bitcast.139, bf16[1536,128]{1,0:T(8,128)(2,1)} %param.22, bf16[1536,128]{1,0:T(8,128)(2,1)} %param.21, bf16[1536,384]{1,0:T(8,128)(2,1)} %param.20), kind=kOutput, calls=%fused_computation.17 | convolution fusion | flops 1012531200 | bytes 4849664 | tf_op jit(solution)/shard_map/dot_general | solution.py:216
  34.5 1.5 broadcast_in_dim.49
  36.0 6.1 %all-to-all-start.1 = ((bf16[8,4,512,64]{2,3,1,0:T(8,128)(2,1)}), bf16[8,4,512,64]{2,3,1,0:T(8,128)(2,1)}, u32[]{:S(2)}, u32[]{:S(2)}) async-start(bf16[8,4,512,64]{2,3,1,0:T(8,128)(2,1)} %broadcast_in_dim.49), calls=%async_computation.1 | async-start | bytes 4194304 | tf_op jit(solution)/shard_map/all_to_all | solution.py:55
  44.6 1.2 slice.79
  46.9 1.3 maximum_bitcast_fusion.q_ref
  48.2 39.1 %all-to-all-done.1 = bf16[8,4,512,64]{2,3,1,0:T(8,128)(2,1)} async-done(((bf16[8,4,512,64]{2,3,1,0:T(8,128)(2,1)}), bf16[8,4,512,64]{2,3,1,0:T(8,128)(2,1)}, u32[]{:S(2)}, u32[]{:S(2)}) %all-to-all-start.1) | async-done | bytes 2097184 | tf_op jit(solution)/shard_map/all_to_all | solution.py:55
  87.4 4.9 %copy.93 = bf16[4,8,512,64]{3,2,1,0:T(8,128)(2,1)} copy(bf16[4,8,512,64]{2,3,0,1:T(8,128)(2,1)} %bitcast.19) | data formatting | bytes 4194304 | tf_op jit(solution)/shard_map/transpose | solution.py:56
  92.2 34.1 %shard_map.157 = bf16[2,3,512,64]{3,2,1,0:T(8,128)(2,1)} custom-call(s32[4]{0:T(128)} %get-tuple-element.34.lo_ref, s32[4]{0:T(128)} %get-tuple-element.33.hi_ref, bf16[2,3,512,64]{3,2,1,0:T(8,128)(2,1)} %maximum_bitcast_fusion.q_ref, bf16[4,4096,64]{2,1,0:T(8,128)(2,1)} %bitcast.126, bf16[4,4096,64]{2,1,0:T(8,128)(2,1)} %bitcast.127, ...), custom_call_target="tpu_custom_call" | custom-call | tf_op jit(solution)/shard_map/pallas_call | solution.py:181
  126.3 1.4 copy.95
  128.9 2.4 %collective-permute-done.2 = bf16[2,128,1536]{2,1,0:T(8,128)(2,1)} collective-permute-done((bf16[2,128,1536]{2,1,0:T(8,128)(2,1)S(1)}, bf16[2,128,1536]{2,1,0:T(8,128)(2,1)}, u32[]{:S(2)}, u32[]{:S(2)}) %collective-permute-start.2) | collective-permute-done | bytes 786464 | tf_op jit(solution)/shard_map/ppermute | solution.py:105
  131.3 1.4 convert_add_fusion.1
  133.9 1.5 collective-permute-start.3
  135.5 9.7 %collective-permute-done.3 = bf16[128,1536]{1,0:T(8,128)(2,1)S(1)} collective-permute-done((bf16[128,1536]{1,0:T(8,128)(2,1)S(1)}, bf16[128,1536]{1,0:T(8,128)(2,1)S(1)}, u32[]{:S(2)}, u32[]{:S(2)}) %collective-permute-start.3) | collective-permute-done | bytes 393248 | tf_op jit(solution)/shard_map/ppermute | solution.py:110
  145.1 1.4 multiply_reduce_fusion
  147.5 1.5 collective-permute-start.4
  149.7 3.5 %all-to-all-start.2 = ((f32[4,128,40]{1,2,0:T(8,128)}), f32[4,128,40]{1,2,0:T(8,128)S(1)}, u32[]{:S(2)}, u32[]{:S(2)}) async-start(f32[4,128,40]{1,2,0:T(8,128)} %broadcast_in_dim.53), calls=%async_computation.2 | async-start | bytes 163840 | tf_op jit(solution)/shard_map/all_to_all | solution.py:55
  153.3 5.0 %collective-permute-done.4 = bf16[128,1536]{1,0:T(8,128)(2,1)S(1)} collective-permute-done((bf16[128,1536]{1,0:T(8,128)(2,1)S(1)}, bf16[128,1536]{1,0:T(8,128)(2,1)S(1)}, u32[]{:S(2)}, u32[]{:S(2)}) %collective-permute-start.4) | collective-permute-done | bytes 393248 | tf_op jit(solution)/shard_map/ppermute | solution.py:84
  159.5 1.3 collective-permute-done.5
  161.0 1.9 gather_fusion.1
  162.9 17.3 %fusion.4 = f32[10,192,1024]{2,1,0:T(8,128)} fusion(bf16[10,1536,1024]{2,1,0:T(8,128)(2,1)} %param.24, bf16[512,1536,1]{1,0,2:T(8,128)(2,1)} %bitcast.138, s32[10,512]{1,0:T(8,128)S(1)} %copy.100, pred[10,512]{1,0:T(8,128)(4,1)S(1)} %get-tuple-element.17), kind=kOutput, calls=%fused_computation.6 | convolution fusion | flops 9064611840 | bytes 40920064 | tf_op jit(solution)/shard_map/esd,edf->esf/dot_general | solution.py:289
  180.2 14.5 %fusion.17 = bf16[512,1536]{1,0:T(8,128)(2,1)S(1)} fusion(bf16[10,512,1536]{2,1,0:T(8,128)(2,1)} %param.25, f32[10,192,1024]{2,1,0:T(8,128)} %fusion.4, bf16[10,512]{1,0:T(8,128)(2,1)S(1)} %dynamic-slice_bitcast_fusion, s32[10,512]{1,0:T(8,128)S(1)} %copy.100, pred[10,512]{1,0:T(8,128)(4,1)S(1)} %get-tuple-element.17), kind=kOutput, calls=%fused_computation.16 | convolution fusion | flops 6052380672 | bytes 25201664 | tf_op jit(solution)/shard_map/esr,esd->rd/dot_general | solution.py:297
  198.6 1.5 collective-permute-start.7
  200.2 2.9 %gather_fusion.2 = bf16[12,2,2,64,64]{4,3,2,1,0:T(8,128)(2,1)S(1)} fusion(bf16[2,2,64,64,64]{4,3,2,1,0:T(8,128)(2,1)} %bitcast.128, s32[1024]{0:T(1024)S(1)} %pad_clamp_fusion), kind=kCustom, calls=%fused_computation.2 | custom fusion | bytes 786480 | tf_op jit(solution)/shard_map/jit(_take)/gather | solution.py:257
  204.2 5.7 %collective-permute-done.7 = bf16[128,1536]{1,0:T(8,128)(2,1)S(1)} collective-permute-done((bf16[128,1536]{1,0:T(8,128)(2,1)S(1)}, bf16[128,1536]{1,0:T(8,128)(2,1)S(1)}, u32[]{:S(2)}, u32[]{:S(2)}) %collective-permute-start.7) | collective-permute-done | bytes 393248 | tf_op jit(solution)/shard_map/ppermute | solution.py:110
  (95 shorter events, 21.3 us)
Async XLA Ops:
  0.6 127.1 %copy-start = (bf16[384,1536]{1,0:T(8,128)(2,1)S(1)}, bf16[384,1536]{1,0:T(8,128)(2,1)}, u32[]{:S(2)}) copy-start(bf16[384,1536]{1,0:T(8,128)(2,1)} %param.23) | copy-start | bytes 3538948
  0.6 11.3 %copy-start.2 = (bf16[128,1536]{1,0:T(8,128)(2,1)S(1)}, bf16[128,1536]{1,0:T(8,128)(2,1)}, u32[]{:S(2)}) copy-start(bf16[128,1536]{1,0:T(8,128)(2,1)} %param.14) | copy-start | bytes 1179652
  2.0 20.6 %all-to-all-start = ((s32[32,1,128]{2,1,0:T(1,128)}), s32[32,1,128]{2,1,0:T(1,128)S(1)}, u32[]{:S(2)}, u32[]{:S(2)}) async-start(s32[32,1,128]{2,1,0:T(1,128)} %broadcast_in_dim.43), calls=%async_computation | async-start | bytes 32768 | tf_op jit(solution)/shard_map/all_to_all | solution.py:55
  10.4 11.2 %collective-permute-start = (bf16[128,1536]{1,0:T(8,128)(2,1)S(1)}, bf16[128,1536]{1,0:T(8,128)(2,1)S(1)}, u32[]{:S(2)}, u32[]{:S(2)}) collective-permute-start(bf16[128,1536]{1,0:T(8,128)(2,1)S(1)} %fusion.40), channel_id=1, source_target_pairs={{0,2},{1,3},{2,0},{3,1},{4,6},{5,7},{6,4},{7,5},{8,10},{9,11},{10,... | collective-permute-start | bytes 1179656 | tf_op jit(solution)/shard_map/ppermute | solution.py:84
  22.6 2.3 %collective-permute-start.1 = (bf16[2,128,1536]{2,1,0:T(8,128)(2,1)S(1)}, bf16[2,128,1536]{2,1,0:T(8,128)(2,1)S(1)}, u32[]{:S(2)}, u32[]{:S(2)}) collective-permute-start(bf16[2,128,1536]{2,1,0:T(8,128)(2,1)S(1)} %get-tuple-element.28), channel_id=1, source_target_pairs={{0,1},{1,0},{2,3},{3,2},{4,5},{5,4},{6,7},{7,6},{8,9},{9,8},{10,11... | collective-permute-start | bytes 2359304 | tf_op jit(solution)/shard_map/ppermute | solution.py:86
  24.9 0.9 copy-start.9
  33.0 1.1 copy-start.7
  36.0 51.3 %all-to-all-start.1 = ((bf16[8,4,512,64]{2,3,1,0:T(8,128)(2,1)}), bf16[8,4,512,64]{2,3,1,0:T(8,128)(2,1)}, u32[]{:S(2)}, u32[]{:S(2)}) async-start(bf16[8,4,512,64]{2,3,1,0:T(8,128)(2,1)} %broadcast_in_dim.49), calls=%async_computation.1 | async-start | bytes 4194304 | tf_op jit(solution)/shard_map/all_to_all | solution.py:55
  128.8 2.5 %collective-permute-start.2 = (bf16[2,128,1536]{2,1,0:T(8,128)(2,1)S(1)}, bf16[2,128,1536]{2,1,0:T(8,128)(2,1)}, u32[]{:S(2)}, u32[]{:S(2)}) collective-permute-start(bf16[2,128,1536]{2,1,0:T(8,128)(2,1)S(1)} %select_bitcast_fusion.1), channel_id=1, source_target_pairs={{0,1},{1,0},{2,3},{3,2},{4,5},{5,4},{6,7},{7,6},{8,9},{9,8},{10,11... | collective-permute-start | bytes 2359304 | tf_op jit(solution)/shard_map/ppermute | solution.py:105
  132.7 1.2 copy-start.3
  133.9 12.7 %copy-start.10 = (f32[1536]{0:T(1024)S(1)}, f32[1536]{0:T(1024)}, u32[]{:S(2)}) copy-start(f32[1536]{0:T(1024)} %param.19) | copy-start | bytes 18436
  133.9 12.7 %copy-start.4 = (f32[2,128,1536]{2,1,0:T(8,128)S(1)}, f32[2,128,1536]{2,1,0:T(8,128)}, u32[]{:S(2)}) copy-start(f32[2,128,1536]{2,1,0:T(8,128)} %copy-done.3) | copy-start | bytes 4718596
  133.9 11.2 %collective-permute-start.3 = (bf16[128,1536]{1,0:T(8,128)(2,1)S(1)}, bf16[128,1536]{1,0:T(8,128)(2,1)S(1)}, u32[]{:S(2)}, u32[]{:S(2)}) collective-permute-start(bf16[128,1536]{1,0:T(8,128)(2,1)S(1)} %fusion.42), channel_id=1, source_target_pairs={{0,2},{1,3},{2,0},{3,1},{4,6},{5,7},{6,4},{7,5},{8,10},{9,11},{10,... | collective-permute-start | bytes 1179656 | tf_op jit(solution)/shard_map/ppermute | solution.py:110
  146.5 2.5 %copy-start.11 = (f32[128,8]{0,1:T(8,128)S(1)}, f32[128,8]{0,1:T(8,128)}, u32[]{:S(2)}) copy-start(f32[128,8]{0,1:T(8,128)} %param.17) | copy-start | bytes 12292
  146.5 2.5 %copy-start.12 = (s32[128,8]{0,1:T(8,128)S(1)}, s32[128,8]{0,1:T(8,128)}, u32[]{:S(2)}) copy-start(s32[128,8]{0,1:T(8,128)} %param.16) | copy-start | bytes 12292
  147.5 10.8 %collective-permute-start.4 = (bf16[128,1536]{1,0:T(8,128)(2,1)S(1)}, bf16[128,1536]{1,0:T(8,128)(2,1)S(1)}, u32[]{:S(2)}, u32[]{:S(2)}) collective-permute-start(bf16[128,1536]{1,0:T(8,128)(2,1)S(1)} %get-tuple-element.21), channel_id=1, source_target_pairs={{0,2},{1,3},{2,0},{3,1},{4,6},{5,7},{6,4},{7,5},{8,10},{9,11},{10,... | collective-permute-start | bytes 1179656 | tf_op jit(solution)/shard_map/ppermute | solution.py:84
  149.7 9.1 %all-to-all-start.2 = ((f32[4,128,40]{1,2,0:T(8,128)}), f32[4,128,40]{1,2,0:T(8,128)S(1)}, u32[]{:S(2)}, u32[]{:S(2)}) async-start(f32[4,128,40]{1,2,0:T(8,128)} %broadcast_in_dim.53), calls=%async_computation.2 | async-start | bytes 163840 | tf_op jit(solution)/shard_map/all_to_all | solution.py:55
  158.4 2.4 %collective-permute-start.5 = (bf16[2,128,1536]{2,1,0:T(8,128)(2,1)S(1)}, bf16[2,128,1536]{2,1,0:T(8,128)(2,1)S(1)}, u32[]{:S(2)}, u32[]{:S(2)}) collective-permute-start(bf16[2,128,1536]{2,1,0:T(8,128)(2,1)S(1)} %get-tuple-element.26), channel_id=1, source_target_pairs={{0,1},{1,0},{2,3},{3,2},{4,5},{5,4},{6,7},{7,6},{8,9},{9,8},{10,11... | collective-permute-start | bytes 2359304 | tf_op jit(solution)/shard_map/ppermute | solution.py:86
  194.7 0.7 copy-start.13
  194.8 2.4 %collective-permute-start.6 = (bf16[2,128,1536]{2,1,0:T(8,128)(2,1)S(1)}, bf16[2,128,1536]{2,1,0:T(8,128)(2,1)S(1)}, u32[]{:S(2)}, u32[]{:S(2)}) collective-permute-start(bf16[2,128,1536]{2,1,0:T(8,128)(2,1)S(1)} %select_bitcast_fusion), channel_id=1, source_target_pairs={{0,1},{1,0},{2,3},{3,2},{4,5},{5,4},{6,7},{7,6},{8,9},{9,8},{10,11... | collective-permute-start | bytes 2359304 | tf_op jit(solution)/shard_map/ppermute | solution.py:105
  197.4 1.2 copy-start.5
  198.6 4.5 %copy-start.8 = (bf16[12,2,2,64,64]{4,3,2,1,0:T(8,128)(2,1)S(1)}, bf16[12,2,2,64,64]{4,3,2,1,0:T(8,128)(2,1)}, u32[]{:S(2)}) copy-start(bf16[12,2,2,64,64]{4,3,2,1,0:T(8,128)(2,1)} %param.26) | copy-start | bytes 1179652
  198.6 11.2 %collective-permute-start.7 = (bf16[128,1536]{1,0:T(8,128)(2,1)S(1)}, bf16[128,1536]{1,0:T(8,128)(2,1)S(1)}, u32[]{:S(2)}, u32[]{:S(2)}) collective-permute-start(bf16[128,1536]{1,0:T(8,128)(2,1)S(1)} %fusion.43), channel_id=1, source_target_pairs={{0,2},{1,3},{2,0},{3,1},{4,6},{5,7},{6,4},{7,5},{8,10},{9,11},{10,... | collective-permute-start | bytes 1179656 | tf_op jit(solution)/shard_map/ppermute | solution.py:110
  203.1 6.8 %copy-start.6 = (f32[2,128,1536]{2,1,0:T(8,128)S(1)}, f32[2,128,1536]{2,1,0:T(8,128)}, u32[]{:S(2)}) copy-start(f32[2,128,1536]{2,1,0:T(8,128)} %copy-done.5) | copy-start | bytes 4718596
  203.1 7.6 %copy-start.1 = (bf16[384,1536]{1,0:T(8,128)(2,1)S(1)}, bf16[384,1536]{1,0:T(8,128)(2,1)}, u32[]{:S(2)}) copy-start(bf16[384,1536]{1,0:T(8,128)(2,1)} %param.23) | copy-start | bytes 3538948

commit v2 on v1

--- a/solution.py
+++ b/solution.py
@@ -206,12 +206,12 @@
     ep_count = lax.axis_size("ep")
     group_len = tok_dev * ep_count
     req_pos = lax.axis_index("req")
+    normed = rms_scale(tokens.astype(jnp.float32), norm1_gain).astype(jnp.bfloat16)
+    seg_ids, normed = lax.optimization_barrier((seg_ids, normed))
     all_segs = gather_rows(seg_ids, ("req", "ep"))
     all_pos = positions_of(all_segs)
     group_start = req_pos * group_len
     group_pos = lax.dynamic_slice_in_dim(all_pos, group_start, group_len)
-    group_seg = lax.dynamic_slice_in_dim(all_segs, group_start, group_len)
-    normed = rms_scale(tokens.astype(jnp.float32), norm1_gain).astype(jnp.bfloat16)
     joined = jnp.concatenate([w_query, key_weight, value_weight], axis=1)
     projected = jnp.dot(
         gather_ep(normed), joined, preferred_element_type=jnp.float32

time: 212 us -> 201 us (0.948)
  waiting for transfers between devices: 74.3 us -> 61.9 us
  starting transfers between devices: 22 us -> 18.3 us
  local copies, waits for them, and re-layouts: 25.9 us -> 29 us
  other arithmetic: 17.2 us -> 19.5 us
    all_to_all x3, waiting for transfers between devices: 39.4 us -> 32.5 us  [gather_rows(): got = lax.all_to_all(spread, axis_name, 0, 0, tiled=True)]
    ppermute x2, waiting for transfers between devices: 13.8 us -> 7.85 us  [gather_ep(): side.append(lax.ppermute(x, 'ep', chip_pairs(count, shift)))]
    slice x2, local copies, waits for them, and re-layouts: 1.45 us -> 4.37 us  [body(): projected[:, :query_width].reshape(group_len, q_heads, HEAD_SIZE)]
    another operation x3, local copies, waits for them, and re-layouts: 0.86 us -> 3.34 us
    unnamed x29 -> x35, local copies, waits for them, and re-layouts: 5.54 us -> 4.66 us
  transfers between devices with their start and end apart: 11 -> 11, of which waited for: 10 -> 10; matrix products, arithmetic and copies ran while one was open for 8% -> 13% of each run, Pallas kernels for 0% -> 0%
where the time goes in v2:
time: 201 us; the launch traced here: 200 us
  waiting for transfers between devices  61.9 us (31%)
  matrix products  35.9 us (18%)
  Pallas kernels  34.1 us (17%)
  local copies, waits for them, and re-layouts  29 us (14%)
  other arithmetic  19.5 us (10%)
  starting transfers between devices  18.3 us (9%)
    pallas_call x1, Pallas kernels, flash_attention(): pl.pallas_call(flash_body, grid_spec=grid_spec, out_shape=jax.ShapeDtypeS...  34.1 us
    all_to_all x3, waiting for transfers between devices, gather_rows(): got = lax.all_to_all(spread, axis_name, 0, 0, tiled=True)  32.5 us
    dot_general x1, matrix products, body(): jnp.einsum('esd,edf->esf', arrived, w_in, preferred_element_type=jnp.floa...  17.3 us
    ppermute x2, waiting for transfers between devices, scatter_sum_ep(): lax.ppermute(piece.astype(jnp.bfloat16), 'ep', chip_pairs(count, shift))  17.1 us
    dot_general x1, matrix products, body(): jnp.einsum('esr,esd->rd', combine.astype(jnp.bfloat16), result, preferred...  14.5 us
    all_to_all x3, starting transfers between devices, gather_rows(): got = lax.all_to_all(spread, axis_name, 0, 0, tiled=True)  14.4 us
    ppermute x2, waiting for transfers between devices, gather_ep(): side.append(lax.ppermute(x, 'ep', chip_pairs(count, shift)))  7.85 us
    unnamed x35, local copies, waits for them, and re-layouts  4.66 us
  transfers between devices with their start and end apart: 11, of which 10 were waited for; matrix products, arithmetic and copies ran while one was open for 13% of the time, Pallas kernels for 0%

profile of v2, /device:TPU:12, one launch (start us, length us, event | category | flops | bytes accessed | tf_op | source)
XLA Modules:
  0.0 199.8 jit_solution(3362385180196528200)
XLA Ops:
  0.6 1.3 fusion.38
  3.1 1.6 collective-permute-start
  4.6 1.3 broadcast_in_dim.43
  5.9 5.1 %all-to-all-start = ((s32[32,1,128]{2,1,0:T(1,128)}), s32[32,1,128]{2,1,0:T(1,128)S(1)}, u32[]{:S(2)}, u32[]{:S(2)}) async-start(s32[32,1,128]{2,1,0:T(1,128)} %broadcast_in_dim.43), calls=%async_computation | async-start | bytes 32768 | tf_op jit(solution)/shard_map/all_to_all | solution.py:55
  12.1 1.9 collective-permute-done
  14.2 1.7 all-to-all-done
  16.7 1.6 multiply_cosine_fusion
  18.3 1.6 maximum_select_fusion
  19.9 2.1 %gather_fusion = bf16[2,2,128,1536]{3,2,1,0:T(8,128)(2,1)} fusion(bf16[2,2,128,1536]{3,2,0,1:T(8,128)(2,1)S(1)} %maximum_select_fusion, s32[1024]{0:T(1024)} %pad_clamp_fusion.1), kind=kCustom, calls=%fused_computation | custom fusion | bytes 3145736 | tf_op jit(solution)/shard_map/jit(_take)/gather | solution.py:89
  22.0 3.1 %fusion.22 = f32[512,640]{1,0:T(8,128)S(1)} fusion(bf16[512,1536]{1,0:T(8,128)(2,1)} %bitcast.140, bf16[1536,128]{1,0:T(8,128)(2,1)S(1)} %copy-done.15, bf16[1536,128]{1,0:T(8,128)(2,1)S(1)} %copy-done.16, bf16[1536,384]{1,0:T(8,128)(2,1)} %param.20), kind=kOutput, calls=%fused_computation.17 | convolution fusion | flops 1012531200 | bytes 4849664 | tf_op jit(solution)/shard_map/dot_general | solution.py:216
  26.6 1.6 broadcast_in_dim.49
  28.2 5.9 %all-to-all-start.1 = ((bf16[8,4,512,64]{2,3,1,0:T(8,128)(2,1)}), bf16[8,4,512,64]{2,3,1,0:T(8,128)(2,1)S(1)}, u32[]{:S(2)}, u32[]{:S(2)}) async-start(bf16[8,4,512,64]{2,3,1,0:T(8,128)(2,1)} %broadcast_in_dim.49), calls=%async_computation.1 | async-start | bytes 4194304 | tf_op jit(solution)/shard_map/all_to_all | solution.py:55
  36.6 2.1 %slice.79 = f32[512,384]{1,0:T(8,128)} slice(f32[512,640]{1,0:T(8,128)} %copy-done.7), slice={[0:512], [0:384]} | slice | bytes 1572864 | tf_op jit(solution)/shard_map/slice | solution.py:225
  38.6 2.3 %copy.88 = f32[512,384]{0,1:T(8,128)} copy(f32[512,384]{1,0:T(8,128)} %slice.79) | data formatting | bytes 1572864 | tf_op jit(solution)/shard_map/slice | solution.py:225
  40.9 1.9 subtract_convert_fusion
  42.9 2.1 %copy.89 = bf16[512,6,32]{2,0,1:T(8,128)(2,1)} copy(bf16[512,6,32]{0,2,1:T(8,128)(2,1)} %get-tuple-element.27) | data formatting | bytes 393216 | tf_op jit(solution)/shard_map/convert.8
  46.1 2.7 %maximum_bitcast_fusion.q_ref = bf16[2,3,512,64]{3,2,1,0:T(8,128)(2,1)} fusion(bf16[512,2,3,32]{3,0,2,1:T(8,128)(2,1)} %bitcast.135, bf16[512,2,3,32]{3,0,2,1:T(8,128)(2,1)} %bitcast.134), kind=kLoop, calls=%fused_computation.45 | loop fusion | flops 786432 | bytes 786432 | tf_op jit(solution)/shard_map/transpose | solution.py:238
  48.8 30.5 %all-to-all-done.1 = bf16[8,4,512,64]{2,3,1,0:T(8,128)(2,1)S(1)} async-done(((bf16[8,4,512,64]{2,3,1,0:T(8,128)(2,1)}), bf16[8,4,512,64]{2,3,1,0:T(8,128)(2,1)S(1)}, u32[]{:S(2)}, u32[]{:S(2)}) %all-to-all-start.1) | async-done | bytes 2097184 | tf_op jit(solution)/shard_map/all_to_all | solution.py:55
  79.3 3.2 %copy.93 = bf16[4,8,512,64]{3,2,1,0:T(8,128)(2,1)} copy(bf16[4,8,512,64]{2,3,0,1:T(8,128)(2,1)S(1)} %bitcast.130) | data formatting | bytes 4194304 | tf_op jit(solution)/shard_map/transpose | solution.py:56
  82.5 34.1 %shard_map.157 = bf16[2,3,512,64]{3,2,1,0:T(8,128)(2,1)} custom-call(s32[4]{0:T(128)} %get-tuple-element.38.lo_ref, s32[4]{0:T(128)} %get-tuple-element.37.hi_ref, bf16[2,3,512,64]{3,2,1,0:T(8,128)(2,1)} %maximum_bitcast_fusion.q_ref, bf16[4,4096,64]{2,1,0:T(8,128)(2,1)} %bitcast.125, bf16[4,4096,64]{2,1,0:T(8,128)(2,1)} %bitcast.126, ...), custom_call_target="tpu_custom_call" | custom-call | tf_op jit(solution)/shard_map/pallas_call | solution.py:181
  116.6 1.4 copy.95
  119.2 2.2 %collective-permute-done.2 = bf16[2,128,1536]{2,1,0:T(8,128)(2,1)S(1)} collective-permute-done((bf16[2,128,1536]{2,1,0:T(8,128)(2,1)S(1)}, bf16[2,128,1536]{2,1,0:T(8,128)(2,1)S(1)}, u32[]{:S(2)}, u32[]{:S(2)}) %collective-permute-start.2) | collective-permute-done | bytes 786464 | tf_op jit(solution)/shard_map/ppermute | solution.py:105
  123.6 10.6 %collective-permute-done.3 = bf16[128,1536]{1,0:T(8,128)(2,1)S(1)} collective-permute-done((bf16[128,1536]{1,0:T(8,128)(2,1)S(1)}, bf16[128,1536]{1,0:T(8,128)(2,1)S(1)}, u32[]{:S(2)}, u32[]{:S(2)}) %collective-permute-start.3) | collective-permute-done | bytes 393248 | tf_op jit(solution)/shard_map/ppermute | solution.py:110
  134.2 1.4 multiply_reduce_fusion
  137.9 3.5 %all-to-all-start.2 = ((f32[4,128,40]{1,2,0:T(8,128)}), f32[4,128,40]{1,2,0:T(8,128)S(1)}, u32[]{:S(2)}, u32[]{:S(2)}) async-start(f32[4,128,40]{1,2,0:T(8,128)} %broadcast_in_dim.53), calls=%async_computation.2 | async-start | bytes 163840 | tf_op jit(solution)/shard_map/all_to_all | solution.py:55
  141.4 5.9 %collective-permute-done.4 = bf16[128,1536]{1,0:T(8,128)(2,1)S(1)} collective-permute-done((bf16[128,1536]{1,0:T(8,128)(2,1)S(1)}, bf16[128,1536]{1,0:T(8,128)(2,1)S(1)}, u32[]{:S(2)}, u32[]{:S(2)}) %collective-permute-start.4) | collective-permute-done | bytes 393248 | tf_op jit(solution)/shard_map/ppermute | solution.py:84
  148.5 1.3 collective-permute-done.5
  150.1 2.0 gather_fusion.1
  152.1 17.3 %fusion.4 = f32[10,192,1024]{2,1,0:T(8,128)} fusion(bf16[10,1536,1024]{2,1,0:T(8,128)(2,1)} %param.24, bf16[512,1536,1]{1,0,2:T(8,128)(2,1)} %bitcast.139, s32[10,512]{1,0:T(8,128)S(1)} %copy.100, pred[10,512]{1,0:T(8,128)(4,1)S(1)} %get-tuple-element.21), kind=kOutput, calls=%fused_computation.6 | convolution fusion | flops 9064611840 | bytes 40920064 | tf_op jit(solution)/shard_map/esd,edf->esf/dot_general | solution.py:289
  169.4 14.5 %fusion.17 = bf16[512,1536]{1,0:T(8,128)(2,1)S(1)} fusion(bf16[10,512,1536]{2,1,0:T(8,128)(2,1)} %param.25, f32[10,192,1024]{2,1,0:T(8,128)} %fusion.4, bf16[10,512]{1,0:T(8,128)(2,1)S(1)} %dynamic-slice_bitcast_fusion, s32[10,512]{1,0:T(8,128)S(1)} %copy.100, pred[10,512]{1,0:T(8,128)(4,1)S(1)} %get-tuple-element.21), kind=kOutput, calls=%fused_computation.16 | convolution fusion | flops 6052380672 | bytes 25201664 | tf_op jit(solution)/shard_map/esr,esd->rd/dot_general | solution.py:297
  188.5 2.9 %gather_fusion.2 = bf16[12,2,2,64,64]{4,3,2,1,0:T(8,128)(2,1)S(1)} fusion(bf16[2,2,64,64,64]{4,3,2,1,0:T(8,128)(2,1)} %bitcast.127, s32[1024]{0:T(1024)S(1)} %pad_clamp_fusion), kind=kCustom, calls=%fused_computation.2 | custom fusion | bytes 786480 | tf_op jit(solution)/shard_map/jit(_take)/gather | solution.py:257
  192.5 6.5 %collective-permute-done.7 = bf16[128,1536]{1,0:T(8,128)(2,1)S(1)} collective-permute-done((bf16[128,1536]{1,0:T(8,128)(2,1)S(1)}, bf16[128,1536]{1,0:T(8,128)(2,1)S(1)}, u32[]{:S(2)}, u32[]{:S(2)}) %collective-permute-start.7) | collective-permute-done | bytes 393248 | tf_op jit(solution)/shard_map/ppermute | solution.py:110
  (100 shorter events, 21.8 us)
Async XLA Ops:
  0.6 117.4 %copy-start = (bf16[384,1536]{1,0:T(8,128)(2,1)S(1)}, bf16[384,1536]{1,0:T(8,128)(2,1)}, u32[]{:S(2)}) copy-start(bf16[384,1536]{1,0:T(8,128)(2,1)} %param.23) | copy-start | bytes 3538948
  3.1 11.0 %collective-permute-start = (bf16[128,1536]{1,0:T(8,128)(2,1)S(1)}, bf16[128,1536]{1,0:T(8,128)(2,1)S(1)}, u32[]{:S(2)}, u32[]{:S(2)}) collective-permute-start(bf16[128,1536]{1,0:T(8,128)(2,1)S(1)} %fusion.40), channel_id=1, source_target_pairs={{0,2},{1,3},{2,0},{3,1},{4,6},{5,7},{6,4},{7,5},{8,10},{9,11},{10,... | collective-permute-start | bytes 1179656 | tf_op jit(solution)/shard_map/ppermute | solution.py:84
  5.9 10.0 %all-to-all-start = ((s32[32,1,128]{2,1,0:T(1,128)}), s32[32,1,128]{2,1,0:T(1,128)S(1)}, u32[]{:S(2)}, u32[]{:S(2)}) async-start(s32[32,1,128]{2,1,0:T(1,128)} %broadcast_in_dim.43), calls=%async_computation | async-start | bytes 32768 | tf_op jit(solution)/shard_map/all_to_all | solution.py:55
  14.2 4.2 %collective-permute-start.1 = (bf16[2,128,1536]{2,1,0:T(8,128)(2,1)S(1)}, bf16[2,128,1536]{2,1,0:T(8,128)(2,1)}, u32[]{:S(2)}, u32[]{:S(2)}) collective-permute-start(bf16[2,128,1536]{2,1,0:T(8,128)(2,1)S(1)} %get-tuple-element.32), channel_id=1, source_target_pairs={{0,1},{1,0},{2,3},{3,2},{4,5},{5,4},{6,7},{7,6},{8,9},{9,8},{10,11... | collective-permute-start | bytes 2359304 | tf_op jit(solution)/shard_map/ppermute | solution.py:86
  19.9 2.1 %copy-start.15 = (bf16[1536,128]{1,0:T(8,128)(2,1)S(1)}, bf16[1536,128]{1,0:T(8,128)(2,1)}, u32[]{:S(2)}) copy-start(bf16[1536,128]{1,0:T(8,128)(2,1)} %param.22) | copy-start | bytes 1179652
  19.9 2.1 %copy-start.16 = (bf16[1536,128]{1,0:T(8,128)(2,1)S(1)}, bf16[1536,128]{1,0:T(8,128)(2,1)}, u32[]{:S(2)}) copy-start(bf16[1536,128]{1,0:T(8,128)(2,1)} %param.21) | copy-start | bytes 1179652
  25.1 1.1 copy-start.7
  25.1 1.3 copy-start.9
  25.2 1.3 copy-start.10
  28.2 51.2 %all-to-all-start.1 = ((bf16[8,4,512,64]{2,3,1,0:T(8,128)(2,1)}), bf16[8,4,512,64]{2,3,1,0:T(8,128)(2,1)S(1)}, u32[]{:S(2)}, u32[]{:S(2)}) async-start(bf16[8,4,512,64]{2,3,1,0:T(8,128)(2,1)} %broadcast_in_dim.49), calls=%async_computation.1 | async-start | bytes 4194304 | tf_op jit(solution)/shard_map/all_to_all | solution.py:55
  119.1 2.4 %collective-permute-start.2 = (bf16[2,128,1536]{2,1,0:T(8,128)(2,1)S(1)}, bf16[2,128,1536]{2,1,0:T(8,128)(2,1)S(1)}, u32[]{:S(2)}, u32[]{:S(2)}) collective-permute-start(bf16[2,128,1536]{2,1,0:T(8,128)(2,1)S(1)} %select_bitcast_fusion.1), channel_id=1, source_target_pairs={{0,1},{1,0},{2,3},{3,2},{4,5},{5,4},{6,7},{7,6},{8,9},{9,8},{10,11... | collective-permute-start | bytes 2359304 | tf_op jit(solution)/shard_map/ppermute | solution.py:105
  119.2 15.0 %copy-start.4 = (bf16[128,1536]{1,0:T(8,128)(2,1)S(1)}, bf16[128,1536]{1,0:T(8,128)(2,1)}, u32[]{:S(2)}) copy-start(bf16[128,1536]{1,0:T(8,128)(2,1)} %param.14) | copy-start | bytes 1179652
  121.8 1.2 copy-start.2
  122.9 12.7 %copy-start.11 = (f32[1536]{0:T(1024)S(1)}, f32[1536]{0:T(1024)}, u32[]{:S(2)}) copy-start(f32[1536]{0:T(1024)} %param.19) | copy-start | bytes 18436
  123.0 12.7 %copy-start.3 = (f32[2,128,1536]{2,1,0:T(8,128)S(1)}, f32[2,128,1536]{2,1,0:T(8,128)}, u32[]{:S(2)}) copy-start(f32[2,128,1536]{2,1,0:T(8,128)} %copy-done.2) | copy-start | bytes 4718596
  123.0 11.2 %collective-permute-start.3 = (bf16[128,1536]{1,0:T(8,128)(2,1)S(1)}, bf16[128,1536]{1,0:T(8,128)(2,1)S(1)}, u32[]{:S(2)}, u32[]{:S(2)}) collective-permute-start(bf16[128,1536]{1,0:T(8,128)(2,1)S(1)} %fusion.42), channel_id=1, source_target_pairs={{0,2},{1,3},{2,0},{3,1},{4,6},{5,7},{6,4},{7,5},{8,10},{9,11},{10,... | collective-permute-start | bytes 1179656 | tf_op jit(solution)/shard_map/ppermute | solution.py:110
  135.6 1.6 copy-start.12
  135.6 1.6 copy-start.13
  136.6 10.8 %collective-permute-start.4 = (bf16[128,1536]{1,0:T(8,128)(2,1)S(1)}, bf16[128,1536]{1,0:T(8,128)(2,1)S(1)}, u32[]{:S(2)}, u32[]{:S(2)}) collective-permute-start(bf16[128,1536]{1,0:T(8,128)(2,1)S(1)} %get-tuple-element.25), channel_id=1, source_target_pairs={{0,2},{1,3},{2,0},{3,1},{4,6},{5,7},{6,4},{7,5},{8,10},{9,11},{10,... | collective-permute-start | bytes 1179656 | tf_op jit(solution)/shard_map/ppermute | solution.py:84
  137.9 9.9 %all-to-all-start.2 = ((f32[4,128,40]{1,2,0:T(8,128)}), f32[4,128,40]{1,2,0:T(8,128)S(1)}, u32[]{:S(2)}, u32[]{:S(2)}) async-start(f32[4,128,40]{1,2,0:T(8,128)} %broadcast_in_dim.53), calls=%async_computation.2 | async-start | bytes 163840 | tf_op jit(solution)/shard_map/all_to_all | solution.py:55
  147.5 2.4 %collective-permute-start.5 = (bf16[2,128,1536]{2,1,0:T(8,128)(2,1)S(1)}, bf16[2,128,1536]{2,1,0:T(8,128)(2,1)S(1)}, u32[]{:S(2)}, u32[]{:S(2)}) collective-permute-start(bf16[2,128,1536]{2,1,0:T(8,128)(2,1)S(1)} %get-tuple-element.30), channel_id=1, source_target_pairs={{0,1},{1,0},{2,3},{3,2},{4,5},{5,4},{6,7},{7,6},{8,9},{9,8},{10,11... | collective-permute-start | bytes 2359304 | tf_op jit(solution)/shard_map/ppermute | solution.py:86
  183.9 0.7 copy-start.14
  184.0 2.4 %collective-permute-start.6 = (bf16[2,128,1536]{2,1,0:T(8,128)(2,1)S(1)}, bf16[2,128,1536]{2,1,0:T(8,128)(2,1)S(1)}, u32[]{:S(2)}, u32[]{:S(2)}) collective-permute-start(bf16[2,128,1536]{2,1,0:T(8,128)(2,1)S(1)} %select_bitcast_fusion), channel_id=1, source_target_pairs={{0,1},{1,0},{2,3},{3,2},{4,5},{5,4},{6,7},{7,6},{8,9},{9,8},{10,11... | collective-permute-start | bytes 2359304 | tf_op jit(solution)/shard_map/ppermute | solution.py:105
  186.6 1.2 copy-start.5
  187.8 3.6 %copy-start.8 = (bf16[12,2,2,64,64]{4,3,2,1,0:T(8,128)(2,1)S(1)}, bf16[12,2,2,64,64]{4,3,2,1,0:T(8,128)(2,1)}, u32[]{:S(2)}) copy-start(bf16[12,2,2,64,64]{4,3,2,1,0:T(8,128)(2,1)} %param.26) | copy-start | bytes 1179652
  187.8 11.2 %collective-permute-start.7 = (bf16[128,1536]{1,0:T(8,128)(2,1)S(1)}, bf16[128,1536]{1,0:T(8,128)(2,1)S(1)}, u32[]{:S(2)}, u32[]{:S(2)}) collective-permute-start(bf16[128,1536]{1,0:T(8,128)(2,1)S(1)} %fusion.43), channel_id=1, source_target_pairs={{0,2},{1,3},{2,0},{3,1},{4,6},{5,7},{6,4},{7,5},{8,10},{9,11},{10,... | collective-permute-start | bytes 1179656 | tf_op jit(solution)/shard_map/ppermute | solution.py:110
  191.4 7.7 %copy-start.6 = (f32[2,128,1536]{2,1,0:T(8,128)S(1)}, f32[2,128,1536]{2,1,0:T(8,128)}, u32[]{:S(2)}) copy-start(f32[2,128,1536]{2,1,0:T(8,128)} %copy-done.5) | copy-start | bytes 4718596
  191.4 8.5 %copy-start.1 = (bf16[384,1536]{1,0:T(8,128)(2,1)S(1)}, bf16[384,1536]{1,0:T(8,128)(2,1)}, u32[]{:S(2)}) copy-start(bf16[384,1536]{1,0:T(8,128)(2,1)} %param.23) | copy-start | bytes 3538948

commit v3 on v2

--- a/solution.py
+++ b/solution.py
@@ -207,14 +207,25 @@
     group_len = tok_dev * ep_count
     req_pos = lax.axis_index("req")
     normed = rms_scale(tokens.astype(jnp.float32), norm1_gain).astype(jnp.bfloat16)
-    seg_ids, normed = lax.optimization_barrier((seg_ids, normed))
+    expert_ids = jnp.arange(E, dtype=jnp.int32)
+    shares = jnp.sum(
+        jnp.where(routes[:, :, None] == expert_ids[None, None, :], route_weights[:, :, None], 0.0),
+        axis=1,
+    )
+    share_cols = -(-E // 128) * 128
+    packed = jnp.concatenate(
+        [normed, jnp.pad(shares, ((0, 0), (0, share_cols - E))).astype(jnp.bfloat16)], axis=1
+    )
+    seg_ids, packed = lax.optimization_barrier((seg_ids, packed))
     all_segs = gather_rows(seg_ids, ("req", "ep"))
     all_pos = positions_of(all_segs)
     group_start = req_pos * group_len
     group_pos = lax.dynamic_slice_in_dim(all_pos, group_start, group_len)
     joined = jnp.concatenate([w_query, key_weight, value_weight], axis=1)
+    rows_packed = gather_ep(packed)
+    shares_all = rows_packed[:, tokens.shape[1] : tokens.shape[1] + E].astype(jnp.float32)
     projected = jnp.dot(
-        gather_ep(normed), joined, preferred_element_type=jnp.float32
+        rows_packed[:, : tokens.shape[1]], joined, preferred_element_type=jnp.float32
     )
     query_width = w_query.shape[1]
     kv_width = key_weight.shape[1]
@@ -266,13 +277,7 @@
     )
     ffe_width = w_out.shape[1]
     exp_here = w_in.shape[0]
-    expert_ids = jnp.arange(E, dtype=jnp.int32)
-    shares = jnp.sum(
-        jnp.where(routes[:, :, None] == expert_ids[None, None, :], route_weights[:, :, None], 0.0),
-        axis=1,
-    )
     rows_all = gather_ep(moe_in)
-    shares_all = gather_rows(shares, "ep")
     first_expert = lax.axis_index("ep") * exp_here
     shares_here = lax.dynamic_slice_in_dim(shares_all, first_expert, exp_here, 1)
     total_rows = rows_all.shape[0]

time: 201 us -> 204 us (1.015)
    ppermute x2, waiting for transfers between devices: 7.85 us -> 13.3 us  [gather_ep(): side.append(lax.ppermute(x, 'ep', chip_pairs(count, shift)))]
    all_to_all x3 -> x2, starting transfers between devices: 14.4 us -> 11.3 us  [gather_rows(): got = lax.all_to_all(spread, axis_name, 0, 0, tiled=True)]
    all_to_all x3 -> x2, waiting for transfers between devices: 32.5 us -> 30.6 us  [gather_rows(): got = lax.all_to_all(spread, axis_name, 0, 0, tiled=True)]
    unnamed x35 -> x36, local copies, waits for them, and re-layouts: 4.66 us -> 5.4 us
  transfers between devices with their start and end apart: 11 -> 10, of which waited for: 10 -> 8; matrix products, arithmetic and copies ran while one was open for 13% -> 12% of each run, Pallas kernels for 0% -> 0%
where the time goes in v3:
time: 204 us; the launch traced here: 203 us
  waiting for transfers between devices  63.9 us (31%)
  matrix products  36 us (18%)
  Pallas kernels  34.1 us (17%)
  local copies, waits for them, and re-layouts  30.1 us (15%)
  other arithmetic  19.5 us (10%)
  starting transfers between devices  18.2 us (9%)
    pallas_call x1, Pallas kernels, flash_attention(): pl.pallas_call(flash_body, grid_spec=grid_spec, out_shape=jax.ShapeDtypeS...  34.1 us
    all_to_all x2, waiting for transfers between devices, gather_rows(): got = lax.all_to_all(spread, axis_name, 0, 0, tiled=True)  30.6 us
    dot_general x1, matrix products, body(): jnp.einsum('esd,edf->esf', arrived, w_in, preferred_element_type=jnp.floa...  17.3 us
    ppermute x2, waiting for transfers between devices, scatter_sum_ep(): lax.ppermute(piece.astype(jnp.bfloat16), 'ep', chip_pairs(count, shift))  15.5 us
    dot_general x1, matrix products, body(): jnp.einsum('esr,esd->rd', combine.astype(jnp.bfloat16), result, preferred...  14.5 us
    ppermute x2, waiting for transfers between devices, gather_ep(): side.append(lax.ppermute(x, 'ep', chip_pairs(count, shift)))  13.3 us
    all_to_all x2, starting transfers between devices, gather_rows(): got = lax.all_to_all(spread, axis_name, 0, 0, tiled=True)  11.3 us
    unnamed x36, local copies, waits for them, and re-layouts  5.4 us
  transfers between devices with their start and end apart: 10, of which 8 were waited for; matrix products, arithmetic and copies ran while one was open for 12% of the time, Pallas kernels for 0%

profile of v3, /device:TPU:12, one launch (start us, length us, event | category | flops | bytes accessed | tf_op | source)
XLA Modules:
  0.0 203.0 jit_solution(2533326601014831594)
XLA Ops:
  0.7 1.3 fusion.40
  2.8 1.2 fusion.42
  4.0 1.6 collective-permute-start
  6.2 5.1 %all-to-all-start = ((s32[32,1,128]{2,1,0:T(1,128)}), s32[32,1,128]{2,1,0:T(1,128)S(1)}, u32[]{:S(2)}, u32[]{:S(2)}) async-start(s32[32,1,128]{2,1,0:T(1,128)} %broadcast_in_dim.47), calls=%async_computation | async-start | bytes 32768 | tf_op jit(solution)/shard_map/all_to_all | solution.py:55
  11.3 4.4 %collective-permute-done = bf16[128,1664]{1,0:T(8,128)(2,1)S(1)} collective-permute-done((bf16[128,1664]{1,0:T(8,128)(2,1)S(1)}, bf16[128,1664]{1,0:T(8,128)(2,1)S(1)}, u32[]{:S(2)}, u32[]{:S(2)}) %collective-permute-start) | collective-permute-done | bytes 426016 | tf_op jit(solution)/shard_map/ppermute | solution.py:84
  17.9 1.3 collective-permute-done.1
  20.1 2.3 %maximum_select_fusion = bf16[2,2,128,1664]{3,2,0,1:T(8,128)(2,1)S(1)} fusion(bf16[2,1,128,1664]{3,2,0,1:T(8,128)(2,1)} %bitcast.140, bf16[2,1,128,1664]{3,2,0,1:T(8,128)(2,1)} %get-tuple-element.24, pred[]{:T(512)S(6)} %eq.32), kind=kLoop, calls=%fused_computation.30 | loop fusion | flops 2555904 | bytes 3407873 | tf_op jit(solution)/shard_map/jit(_where)/select_n | solution.py:87
  22.4 1.9 gather_fusion
  24.3 3.2 %fusion.22 = f32[512,640]{1,0:T(8,128)S(1)} fusion(bf16[1536,128]{1,0:T(8,128)(2,1)S(1)} %copy-done.16, bf16[1536,128]{1,0:T(8,128)(2,1)} %param.21, bf16[1536,384]{1,0:T(8,128)(2,1)} %param.20, bf16[512,1664]{1,0:T(8,128)(2,1)} %bitcast.131), kind=kOutput, calls=%fused_computation.17 | convolution fusion | flops 1012531200 | bytes 4849664 | tf_op jit(solution)/shard_map/dot_general | solution.py:227
  29.0 1.6 broadcast_in_dim.50
  30.6 6.2 %all-to-all-start.1 = ((bf16[8,4,512,64]{2,3,1,0:T(8,128)(2,1)}), bf16[8,4,512,64]{2,3,1,0:T(8,128)(2,1)S(1)}, u32[]{:S(2)}, u32[]{:S(2)}) async-start(bf16[8,4,512,64]{2,3,1,0:T(8,128)(2,1)} %broadcast_in_dim.50), calls=%async_computation.1 | async-start | bytes 4194304 | tf_op jit(solution)/shard_map/all_to_all | solution.py:55
  39.3 2.1 %slice.88 = f32[512,384]{1,0:T(8,128)} slice(f32[512,640]{1,0:T(8,128)} %copy-done.7), slice={[0:512], [0:384]} | slice | bytes 1572864 | tf_op jit(solution)/shard_map/slice | solution.py:236
  41.4 2.3 %copy.69 = f32[512,384]{0,1:T(8,128)} copy(f32[512,384]{1,0:T(8,128)} %slice.88) | data formatting | bytes 1572864 | tf_op jit(solution)/shard_map/slice | solution.py:236
  43.7 1.9 subtract_convert_fusion
  45.6 2.1 %copy.70 = bf16[512,6,32]{2,0,1:T(8,128)(2,1)} copy(bf16[512,6,32]{0,2,1:T(8,128)(2,1)} %get-tuple-element.22) | data formatting | bytes 393216 | tf_op jit(solution)/shard_map/convert.8
  48.8 2.7 %maximum_bitcast_fusion.q_ref = bf16[2,3,512,64]{3,2,1,0:T(8,128)(2,1)} fusion(bf16[512,2,3,32]{3,0,2,1:T(8,128)(2,1)} %bitcast.129, bf16[512,2,3,32]{3,0,2,1:T(8,128)(2,1)} %bitcast.128), kind=kLoop, calls=%fused_computation.48 | loop fusion | flops 786432 | bytes 786432 | tf_op jit(solution)/shard_map/transpose | solution.py:249
  51.5 30.6 %all-to-all-done.1 = bf16[8,4,512,64]{2,3,1,0:T(8,128)(2,1)S(1)} async-done(((bf16[8,4,512,64]{2,3,1,0:T(8,128)(2,1)}), bf16[8,4,512,64]{2,3,1,0:T(8,128)(2,1)S(1)}, u32[]{:S(2)}, u32[]{:S(2)}) %all-to-all-start.1) | async-done | bytes 2097184 | tf_op jit(solution)/shard_map/all_to_all | solution.py:55
  82.1 3.2 %copy.74 = bf16[4,8,512,64]{3,2,1,0:T(8,128)(2,1)} copy(bf16[4,8,512,64]{2,3,0,1:T(8,128)(2,1)S(1)} %bitcast.124) | data formatting | bytes 4194304 | tf_op jit(solution)/shard_map/transpose | solution.py:56
  85.3 34.1 %shard_map.157 = bf16[2,3,512,64]{3,2,1,0:T(8,128)(2,1)} custom-call(s32[4]{0:T(128)} %get-tuple-element.35.lo_ref, s32[4]{0:T(128)} %get-tuple-element.34.hi_ref, bf16[2,3,512,64]{3,2,1,0:T(8,128)(2,1)} %maximum_bitcast_fusion.q_ref, bf16[4,4096,64]{2,1,0:T(8,128)(2,1)} %bitcast.119, bf16[4,4096,64]{2,1,0:T(8,128)(2,1)} %bitcast.120, ...), custom_call_target="tpu_custom_call" | custom-call | tf_op jit(solution)/shard_map/pallas_call | solution.py:181
  119.4 1.4 copy.76
  122.0 2.2 %collective-permute-done.2 = bf16[2,128,1536]{2,1,0:T(8,128)(2,1)S(1)} collective-permute-done((bf16[2,128,1536]{2,1,0:T(8,128)(2,1)S(1)}, bf16[2,128,1536]{2,1,0:T(8,128)(2,1)S(1)}, u32[]{:S(2)}, u32[]{:S(2)}) %collective-permute-start.2) | collective-permute-done | bytes 786464 | tf_op jit(solution)/shard_map/ppermute | solution.py:105
  125.7 1.6 collective-permute-start.3
  127.3 9.7 %collective-permute-done.3 = bf16[128,1536]{1,0:T(8,128)(2,1)S(1)} collective-permute-done((bf16[128,1536]{1,0:T(8,128)(2,1)S(1)}, bf16[128,1536]{1,0:T(8,128)(2,1)S(1)}, u32[]{:S(2)}, u32[]{:S(2)}) %collective-permute-start.3) | collective-permute-done | bytes 393248 | tf_op jit(solution)/shard_map/ppermute | solution.py:110
  137.0 1.4 multiply_reduce_fusion
  139.3 1.5 collective-permute-start.4
  140.8 8.8 %collective-permute-done.4 = bf16[128,1536]{1,0:T(8,128)(2,1)S(1)} collective-permute-done((bf16[128,1536]{1,0:T(8,128)(2,1)S(1)}, bf16[128,1536]{1,0:T(8,128)(2,1)S(1)}, u32[]{:S(2)}, u32[]{:S(2)}) %collective-permute-start.4) | collective-permute-done | bytes 393248 | tf_op jit(solution)/shard_map/ppermute | solution.py:84
  152.8 2.1 %gather_fusion.1 = bf16[2,2,128,1536]{3,2,1,0:T(8,128)(2,1)} fusion(bf16[2,2,128,1536]{3,2,0,1:T(8,128)(2,1)S(1)} %maximum_select_fusion.1, s32[1024]{0:T(1024)} %copy-done.13), kind=kCustom, calls=%fused_computation.1 | custom fusion | bytes 3145736 | tf_op jit(solution)/shard_map/jit(_take)/gather | solution.py:89
  154.9 17.3 %fusion.4 = f32[10,192,1024]{2,1,0:T(8,128)} fusion(bf16[10,1536,1024]{2,1,0:T(8,128)(2,1)} %param.24, bf16[512,1536,1]{1,0,2:T(8,128)(2,1)} %bitcast.135, s32[10,512]{1,0:T(8,128)S(1)} %copy.79, pred[10,512]{1,0:T(8,128)(4,1)S(1)} %copy-done.12), kind=kOutput, calls=%fused_computation.6 | convolution fusion | flops 9064611840 | bytes 40920064 | tf_op jit(solution)/shard_map/esd,edf->esf/dot_general | solution.py:294
  172.2 14.5 %fusion.17 = bf16[512,1536]{1,0:T(8,128)(2,1)S(1)} fusion(bf16[10,512,1536]{2,1,0:T(8,128)(2,1)} %param.25, f32[10,192,1024]{2,1,0:T(8,128)} %fusion.4, bf16[10,512]{1,0:T(8,128)(2,1)S(1)} %copy.81, s32[10,512]{1,0:T(8,128)S(1)} %copy.79, pred[10,512]{1,0:T(8,128)(4,1)S(1)} %copy-done.12), kind=kOutput, calls=%fused_computation.16 | convolution fusion | flops 6052380672 | bytes 25201664 | tf_op jit(solution)/shard_map/esr,esd->rd/dot_general | solution.py:302
  190.7 1.6 collective-permute-start.7
  192.3 2.9 %gather_fusion.2 = bf16[12,2,2,64,64]{4,3,2,1,0:T(8,128)(2,1)S(1)} fusion(bf16[2,2,64,64,64]{4,3,2,1,0:T(8,128)(2,1)} %bitcast.121, s32[1024]{0:T(1024)S(1)} %pad_clamp_fusion), kind=kCustom, calls=%fused_computation.2 | custom fusion | bytes 786480 | tf_op jit(solution)/shard_map/jit(_take)/gather | solution.py:268
  196.3 5.9 %collective-permute-done.7 = bf16[128,1536]{1,0:T(8,128)(2,1)S(1)} collective-permute-done((bf16[128,1536]{1,0:T(8,128)(2,1)S(1)}, bf16[128,1536]{1,0:T(8,128)(2,1)S(1)}, u32[]{:S(2)}, u32[]{:S(2)}) %collective-permute-start.7) | collective-permute-done | bytes 393248 | tf_op jit(solution)/shard_map/ppermute | solution.py:110
  (100 shorter events, 22.2 us)
Async XLA Ops:
  0.6 120.2 %copy-start = (bf16[384,1536]{1,0:T(8,128)(2,1)S(1)}, bf16[384,1536]{1,0:T(8,128)(2,1)}, u32[]{:S(2)}) copy-start(bf16[384,1536]{1,0:T(8,128)(2,1)} %param.23) | copy-start | bytes 3538948
  0.6 4.9 %copy-start.14 = (s32[128]{0:T(128)S(1)}, s32[128]{0:T(128)}, u32[]{:S(2)}) copy-start(s32[128]{0:T(128)} %param.15) | copy-start | bytes 1540
  4.0 11.8 %collective-permute-start = (bf16[128,1664]{1,0:T(8,128)(2,1)S(1)}, bf16[128,1664]{1,0:T(8,128)(2,1)S(1)}, u32[]{:S(2)}, u32[]{:S(2)}) collective-permute-start(bf16[128,1664]{1,0:T(8,128)(2,1)S(1)} %fusion.44), channel_id=1, source_target_pairs={{0,2},{1,3},{2,0},{3,1},{4,6},{5,7},{6,4},{7,5},{8,10},{9,11},{10,... | collective-permute-start | bytes 1277960 | tf_op jit(solution)/shard_map/ppermute | solution.py:84
  6.2 10.6 %all-to-all-start = ((s32[32,1,128]{2,1,0:T(1,128)}), s32[32,1,128]{2,1,0:T(1,128)S(1)}, u32[]{:S(2)}, u32[]{:S(2)}) async-start(s32[32,1,128]{2,1,0:T(1,128)} %broadcast_in_dim.47), calls=%async_computation | async-start | bytes 32768 | tf_op jit(solution)/shard_map/all_to_all | solution.py:55
  11.3 11.0 %copy-start.13 = (s32[1024]{0:T(1024)}, s32[1024]{0:T(1024)S(1)}, u32[]{:S(2)}) copy-start(s32[1024]{0:T(1024)S(1)} %pad_clamp_fusion.1) | copy-start | bytes 12292
  16.8 2.4 %collective-permute-start.1 = (bf16[2,128,1664]{2,1,0:T(8,128)(2,1)S(1)}, bf16[2,128,1664]{2,1,0:T(8,128)(2,1)S(1)}, u32[]{:S(2)}, u32[]{:S(2)}) collective-permute-start(bf16[2,128,1664]{2,1,0:T(8,128)(2,1)S(1)} %get-tuple-element.25), channel_id=1, source_target_pairs={{0,1},{1,0},{2,3},{3,2},{4,5},{5,4},{6,7},{7,6},{8,9},{9,8},{10,11... | collective-permute-start | bytes 2555912 | tf_op jit(solution)/shard_map/ppermute | solution.py:86
  17.9 11.0 %copy-start.10 = (f32[512,32]{0,1:T(8,128)}, f32[512,32]{0,1:T(8,128)S(1)}, u32[]{:S(2)}) copy-start(f32[512,32]{0,1:T(8,128)S(1)} %get-tuple-element.33) | copy-start | bytes 196612
  19.1 0.9 copy-start.8
  22.3 1.9 copy-start.16
  27.5 1.1 copy-start.7
  30.6 51.5 %all-to-all-start.1 = ((bf16[8,4,512,64]{2,3,1,0:T(8,128)(2,1)}), bf16[8,4,512,64]{2,3,1,0:T(8,128)(2,1)S(1)}, u32[]{:S(2)}, u32[]{:S(2)}) async-start(bf16[8,4,512,64]{2,3,1,0:T(8,128)(2,1)} %broadcast_in_dim.50), calls=%async_computation.1 | async-start | bytes 4194304 | tf_op jit(solution)/shard_map/all_to_all | solution.py:55
  121.9 2.4 %collective-permute-start.2 = (bf16[2,128,1536]{2,1,0:T(8,128)(2,1)S(1)}, bf16[2,128,1536]{2,1,0:T(8,128)(2,1)S(1)}, u32[]{:S(2)}, u32[]{:S(2)}) collective-permute-start(bf16[2,128,1536]{2,1,0:T(8,128)(2,1)S(1)} %select_bitcast_fusion.1), channel_id=1, source_target_pairs={{0,1},{1,0},{2,3},{3,2},{4,5},{5,4},{6,7},{7,6},{8,9},{9,8},{10,11... | collective-permute-start | bytes 2359304 | tf_op jit(solution)/shard_map/ppermute | solution.py:105
  122.0 15.0 %copy-start.4 = (bf16[128,1536]{1,0:T(8,128)(2,1)S(1)}, bf16[128,1536]{1,0:T(8,128)(2,1)}, u32[]{:S(2)}) copy-start(bf16[128,1536]{1,0:T(8,128)(2,1)} %param.14) | copy-start | bytes 1179652
  124.5 1.2 copy-start.2
  125.7 12.7 %copy-start.11 = (f32[1536]{0:T(1024)S(1)}, f32[1536]{0:T(1024)}, u32[]{:S(2)}) copy-start(f32[1536]{0:T(1024)} %param.19) | copy-start | bytes 18436
  125.7 12.6 %copy-start.3 = (f32[2,128,1536]{2,1,0:T(8,128)S(1)}, f32[2,128,1536]{2,1,0:T(8,128)}, u32[]{:S(2)}) copy-start(f32[2,128,1536]{2,1,0:T(8,128)} %copy-done.2) | copy-start | bytes 4718596
  125.7 11.2 %collective-permute-start.3 = (bf16[128,1536]{1,0:T(8,128)(2,1)S(1)}, bf16[128,1536]{1,0:T(8,128)(2,1)S(1)}, u32[]{:S(2)}, u32[]{:S(2)}) collective-permute-start(bf16[128,1536]{1,0:T(8,128)(2,1)S(1)} %fusion.45), channel_id=1, source_target_pairs={{0,2},{1,3},{2,0},{3,1},{4,6},{5,7},{6,4},{7,5},{8,10},{9,11},{10,... | collective-permute-start | bytes 1179656 | tf_op jit(solution)/shard_map/ppermute | solution.py:110
  139.3 10.3 %collective-permute-start.4 = (bf16[128,1536]{1,0:T(8,128)(2,1)S(1)}, bf16[128,1536]{1,0:T(8,128)(2,1)S(1)}, u32[]{:S(2)}, u32[]{:S(2)}) collective-permute-start(bf16[128,1536]{1,0:T(8,128)(2,1)S(1)} %get-tuple-element.20), channel_id=1, source_target_pairs={{0,2},{1,3},{2,0},{3,1},{4,6},{5,7},{6,4},{7,5},{8,10},{9,11},{10,... | collective-permute-start | bytes 1179656 | tf_op jit(solution)/shard_map/ppermute | solution.py:84
  149.8 2.7 %collective-permute-start.5 = (bf16[2,128,1536]{2,1,0:T(8,128)(2,1)S(1)}, bf16[2,128,1536]{2,1,0:T(8,128)(2,1)S(1)}, u32[]{:S(2)}, u32[]{:S(2)}) collective-permute-start(bf16[2,128,1536]{2,1,0:T(8,128)(2,1)S(1)} %get-tuple-element.27), channel_id=1, source_target_pairs={{0,1},{1,0},{2,3},{3,2},{4,5},{5,4},{6,7},{7,6},{8,9},{9,8},{10,11... | collective-permute-start | bytes 2359304 | tf_op jit(solution)/shard_map/ppermute | solution.py:86
  152.7 2.1 %copy-start.12 = (pred[10,512]{1,0:T(8,128)(4,1)S(1)}, pred[10,512]{1,0:T(8,128)(4,1)}, u32[]{:S(2)}) copy-start(pred[10,512]{1,0:T(8,128)(4,1)} %copy.80) | copy-start | bytes 15364
  186.7 0.7 copy-start.15
  186.8 2.5 %collective-permute-start.6 = (bf16[2,128,1536]{2,1,0:T(8,128)(2,1)S(1)}, bf16[2,128,1536]{2,1,0:T(8,128)(2,1)S(1)}, u32[]{:S(2)}, u32[]{:S(2)}) collective-permute-start(bf16[2,128,1536]{2,1,0:T(8,128)(2,1)S(1)} %select_bitcast_fusion), channel_id=1, source_target_pairs={{0,1},{1,0},{2,3},{3,2},{4,5},{5,4},{6,7},{7,6},{8,9},{9,8},{10,11... | collective-permute-start | bytes 2359304 | tf_op jit(solution)/shard_map/ppermute | solution.py:105
  189.5 1.2 copy-start.5
  190.7 4.5 %copy-start.9 = (bf16[12,2,2,64,64]{4,3,2,1,0:T(8,128)(2,1)S(1)}, bf16[12,2,2,64,64]{4,3,2,1,0:T(8,128)(2,1)}, u32[]{:S(2)}) copy-start(bf16[12,2,2,64,64]{4,3,2,1,0:T(8,128)(2,1)} %param.26) | copy-start | bytes 1179652
  190.7 11.5 %collective-permute-start.7 = (bf16[128,1536]{1,0:T(8,128)(2,1)S(1)}, bf16[128,1536]{1,0:T(8,128)(2,1)S(1)}, u32[]{:S(2)}, u32[]{:S(2)}) collective-permute-start(bf16[128,1536]{1,0:T(8,128)(2,1)S(1)} %fusion.46), channel_id=1, source_target_pairs={{0,2},{1,3},{2,0},{3,1},{4,6},{5,7},{6,4},{7,5},{8,10},{9,11},{10,... | collective-permute-start | bytes 1179656 | tf_op jit(solution)/shard_map/ppermute | solution.py:110
  195.2 7.0 %copy-start.6 = (f32[2,128,1536]{2,1,0:T(8,128)S(1)}, f32[2,128,1536]{2,1,0:T(8,128)}, u32[]{:S(2)}) copy-start(f32[2,128,1536]{2,1,0:T(8,128)} %copy-done.5) | copy-start | bytes 4718596
  195.2 7.8 %copy-start.1 = (bf16[384,1536]{1,0:T(8,128)(2,1)S(1)}, bf16[384,1536]{1,0:T(8,128)(2,1)}, u32[]{:S(2)}) copy-start(bf16[384,1536]{1,0:T(8,128)(2,1)} %param.23) | copy-start | bytes 3538948

commit v4 on v2

--- a/solution.py
+++ b/solution.py
@@ -123,14 +123,17 @@
     q_tile = q_ref.shape[2]
     head_dim = q_ref.shape[3]
     q = q_ref[0].reshape(ratio * q_tile, head_dim)
+    per_group = k_ref.shape[2] // K_TILE
     tok = tok_ref[...]
     begin = begin_ref[...]
 
     def step(kb, carry):
         m_old, l_old, acc_old = carry
-        k0 = pl.multiple_of(kb * K_TILE, K_TILE)
-        k_blk = k_ref[0, pl.ds(k0, K_TILE), :]
-        v_blk = v_ref[0, pl.ds(k0, K_TILE), :]
+        k0 = kb * K_TILE
+        grp = kb // per_group
+        off = pl.multiple_of((kb % per_group) * K_TILE, K_TILE)
+        k_blk = k_ref[grp, 0, pl.ds(off, K_TILE), :]
+        v_blk = v_ref[grp, 0, pl.ds(off, K_TILE), :]
         s = lax.dot_general(
             q, k_blk, (((1,), (1,)), ((), ())), preferred_element_type=jnp.float32
         )
@@ -162,7 +165,7 @@
 
 def flash_attention(query_grouped, kv_all, q_index, q_begin):
     kv_heads, ratio, group_len, head_dim = query_grouped.shape
-    n_rows = kv_all.shape[1]
+    n_grp, _, grp_len, _ = kv_all.shape
     n_q = group_len // Q_TILE
     lo = jnp.min(q_begin.reshape(n_q, Q_TILE), axis=1) // K_TILE
     hi = jnp.max(q_index.reshape(n_q, Q_TILE), axis=1) // K_TILE
@@ -171,8 +174,10 @@
         grid=(kv_heads, n_q),
         in_specs=[
             pl.BlockSpec((1, ratio, Q_TILE, head_dim), lambda g, qb, lo, hi: (g, 0, qb, 0)),
-            pl.BlockSpec((1, n_rows, head_dim), lambda g, qb, lo, hi: (g, 0, 0)),
-            pl.BlockSpec((1, n_rows, head_dim), lambda g, qb, lo, hi: (kv_heads + g, 0, 0)),
+            pl.BlockSpec((n_grp, 1, grp_len, head_dim), lambda g, qb, lo, hi: (0, g, 0, 0)),
+            pl.BlockSpec(
+                (n_grp, 1, grp_len, head_dim), lambda g, qb, lo, hi: (0, kv_heads + g, 0, 0)
+            ),
             pl.BlockSpec((Q_TILE, 1), lambda g, qb, lo, hi: (qb, 0)),
             pl.BlockSpec((Q_TILE, 1), lambda g, qb, lo, hi: (qb, 0)),
         ],
@@ -241,20 +246,24 @@
     kv_local = jnp.concatenate(
         [key_rows.transpose(1, 0, 2), value_rows.transpose(1, 0, 2)], axis=0
     )
-    kv_all = gather_rows(kv_local, "req", axis=1)
-    n_rows = kv_all.shape[1]
+    req_count = lax.axis_size("req")
+    kv_all = lax.all_to_all(
+        jnp.broadcast_to(kv_local[None], (req_count,) + kv_local.shape), "req", 0, 0, tiled=True
+    )
     q_index = group_start + jnp.arange(group_len, dtype=jnp.int32)
     q_begin = q_index - group_pos
     head_out = flash_attention(query_grouped, kv_all, q_index, q_begin)
     pages_here = paged_key_value_cache.shape[0]
     page_first = req_pos * pages_here
-    piece_pages = n_rows // PAGE_TOKENS
+    group_pages = group_len // PAGE_TOKENS
     local_pages = page_first + jnp.arange(pages_here, dtype=jnp.int32)
     match = local_pages[:, None] == page_table[None, :]
     hit = jnp.any(match, axis=1)
     block_of = jnp.argmax(match, axis=1).astype(jnp.int32)
-    kv_paged = kv_all.reshape(2, kv_heads, piece_pages, PAGE_TOKENS, HEAD_SIZE)
-    picked = jnp.take(kv_paged, block_of, axis=2, mode="clip").transpose(2, 1, 0, 3, 4)
+    kv_paged = kv_all.reshape(req_count, 2, kv_heads, group_pages, PAGE_TOKENS, HEAD_SIZE)
+    picked = kv_paged[block_of // group_pages, :, :, block_of % group_pages].transpose(
+        0, 2, 1, 3, 4
+    )
     new_cache = jnp.where(hit[:, None, None, None, None], picked, paged_key_value_cache)
     head_out = head_out.transpose(2, 0, 1, 3).reshape(group_len, query_width)
     attention = scatter_sum_ep(

time: 201 us -> 199 us (0.990)
  Pallas kernels: 34.1 us -> 30.2 us
    all_to_all x0 -> x1, waiting for transfers between devices: none -> 30.5 us  [body(): lax.all_to_all(jnp.broadcast_to(kv_local[None], (req_count,) + kv_local.s...]
    all_to_all x3 -> x2, waiting for transfers between devices: 32.5 us -> 1.95 us  [gather_rows(): got = lax.all_to_all(spread, axis_name, 0, 0, tiled=True)]
    all_to_all x0 -> x1, starting transfers between devices: none -> 5.88 us  [body(): lax.all_to_all(jnp.broadcast_to(kv_local[None], (req_count,) + kv_local.s...]
    all_to_all x3 -> x2, starting transfers between devices: 14.4 us -> 8.54 us  [gather_rows(): got = lax.all_to_all(spread, axis_name, 0, 0, tiled=True)]
    pallas_call x1, Pallas kernels: 34.1 us -> 30.2 us  [flash_attention(): pl.pallas_call(flash_body, grid_spec=grid_spec, out_shape=jax.ShapeDtypeS...]
    all_to_all x0 -> x1, local copies, waits for them, and re-layouts: none -> 3.21 us  [body(): lax.all_to_all(jnp.broadcast_to(kv_local[None], (req_count,) + kv_local.s...]
    transpose x1 -> x0, local copies, waits for them, and re-layouts: 3.21 us -> none  [gather_rows(): got = jnp.moveaxis(got, 0, axis)]
where the time goes in v4:
time: 199 us; the launch traced here: 196 us
  waiting for transfers between devices  61.8 us (31%)
  matrix products  35.9 us (18%)
  Pallas kernels  30.2 us (15%)
  local copies, waits for them, and re-layouts  29.1 us (15%)
  other arithmetic  19.5 us (10%)
  starting transfers between devices  18.3 us (9%)
    all_to_all x1, waiting for transfers between devices, body(): lax.all_to_all(jnp.broadcast_to(kv_local[None], (req_count,) + kv_local.s...  30.5 us
    pallas_call x1, Pallas kernels, flash_attention(): pl.pallas_call(flash_body, grid_spec=grid_spec, out_shape=jax.ShapeDtypeS...  30.2 us
    dot_general x1, matrix products, body(): jnp.einsum('esd,edf->esf', arrived, w_in, preferred_element_type=jnp.floa...  17.3 us
    ppermute x2, waiting for transfers between devices, scatter_sum_ep(): lax.ppermute(piece.astype(jnp.bfloat16), 'ep', chip_pairs(count, shift))  16.9 us
    dot_general x1, matrix products, body(): jnp.einsum('esr,esd->rd', combine.astype(jnp.bfloat16), result, preferred...  14.5 us
    all_to_all x2, starting transfers between devices, gather_rows(): got = lax.all_to_all(spread, axis_name, 0, 0, tiled=True)  8.54 us
    ppermute x2, waiting for transfers between devices, gather_ep(): side.append(lax.ppermute(x, 'ep', chip_pairs(count, shift)))  7.85 us
    all_to_all x1, starting transfers between devices, body(): lax.all_to_all(jnp.broadcast_to(kv_local[None], (req_count,) + kv_local.s...  5.88 us
  transfers between devices with their start and end apart: 11, of which 10 were waited for; matrix products, arithmetic and copies ran while one was open for 13% of the time, Pallas kernels for 0%

profile of v4, /device:TPU:12, one launch (start us, length us, event | category | flops | bytes accessed | tf_op | source)
XLA Modules:
  0.0 196.0 jit_solution(9522624201311389429)
XLA Ops:
  0.6 1.3 fusion.38
  3.1 1.6 collective-permute-start
  4.6 1.3 broadcast_in_dim.43
  5.9 5.1 %all-to-all-start = ((s32[32,1,128]{2,1,0:T(1,128)}), s32[32,1,128]{2,1,0:T(1,128)S(1)}, u32[]{:S(2)}, u32[]{:S(2)}) async-start(s32[32,1,128]{2,1,0:T(1,128)} %broadcast_in_dim.43), calls=%async_computation | async-start | bytes 32768 | tf_op jit(solution)/shard_map/all_to_all | solution.py:55
  12.1 1.9 collective-permute-done
  14.2 1.7 all-to-all-done
  16.7 1.6 multiply_cosine_fusion
  18.3 1.6 maximum_select_fusion
  19.9 2.1 %gather_fusion = bf16[2,2,128,1536]{3,2,1,0:T(8,128)(2,1)} fusion(bf16[2,2,128,1536]{3,2,0,1:T(8,128)(2,1)S(1)} %maximum_select_fusion, s32[1024]{0:T(1024)} %pad_clamp_fusion), kind=kCustom, calls=%fused_computation | custom fusion | bytes 3145736 | tf_op jit(solution)/shard_map/jit(_take)/gather | solution.py:89
  22.0 3.1 %fusion.22 = f32[512,640]{1,0:T(8,128)S(1)} fusion(bf16[512,1536]{1,0:T(8,128)(2,1)} %bitcast.135, bf16[1536,128]{1,0:T(8,128)(2,1)S(1)} %copy-done.15, bf16[1536,128]{1,0:T(8,128)(2,1)S(1)} %copy-done.16, bf16[1536,384]{1,0:T(8,128)(2,1)} %param.20), kind=kOutput, calls=%fused_computation.17 | convolution fusion | flops 1012531200 | bytes 4849664 | tf_op jit(solution)/shard_map/dot_general | solution.py:221
  26.6 1.6 broadcast_in_dim.49
  28.2 5.9 %all-to-all-start.1 = ((bf16[8,4,512,64]{2,3,1,0:T(8,128)(2,1)}), bf16[8,4,512,64]{2,3,1,0:T(8,128)(2,1)S(1)}, u32[]{:S(2)}, u32[]{:S(2)}) async-start(bf16[8,4,512,64]{2,3,1,0:T(8,128)(2,1)} %broadcast_in_dim.49), calls=%async_computation.1 | async-start | bytes 4194304 | tf_op jit(solution)/shard_map/all_to_all | solution.py:250
  36.6 2.1 %slice.79 = f32[512,384]{1,0:T(8,128)} slice(f32[512,640]{1,0:T(8,128)} %copy-done.7), slice={[0:512], [0:384]} | slice | bytes 1572864 | tf_op jit(solution)/shard_map/slice | solution.py:230
  38.6 2.3 %copy.92 = f32[512,384]{0,1:T(8,128)} copy(f32[512,384]{1,0:T(8,128)} %slice.79) | data formatting | bytes 1572864 | tf_op jit(solution)/shard_map/slice | solution.py:230
  40.9 1.9 subtract_convert_fusion
  42.9 2.1 %copy.93 = bf16[512,6,32]{2,0,1:T(8,128)(2,1)} copy(bf16[512,6,32]{0,2,1:T(8,128)(2,1)} %get-tuple-element.27) | data formatting | bytes 393216 | tf_op jit(solution)/shard_map/convert.8
  46.1 2.7 %maximum_bitcast_fusion.q_ref = bf16[2,3,512,64]{3,2,1,0:T(8,128)(2,1)} fusion(bf16[512,2,3,32]{3,0,2,1:T(8,128)(2,1)} %bitcast.130, bf16[512,2,3,32]{3,0,2,1:T(8,128)(2,1)} %bitcast.129), kind=kLoop, calls=%fused_computation.45 | loop fusion | flops 786432 | bytes 786432 | tf_op jit(solution)/shard_map/transpose | solution.py:243
  48.8 30.5 %all-to-all-done.1 = bf16[8,4,512,64]{2,3,1,0:T(8,128)(2,1)S(1)} async-done(((bf16[8,4,512,64]{2,3,1,0:T(8,128)(2,1)}), bf16[8,4,512,64]{2,3,1,0:T(8,128)(2,1)S(1)}, u32[]{:S(2)}, u32[]{:S(2)}) %all-to-all-start.1) | async-done | bytes 2097184 | tf_op jit(solution)/shard_map/all_to_all | solution.py:250
  79.3 3.2 %copy.97.k_ref.v_ref = bf16[8,4,512,64]{3,2,1,0:T(8,128)(2,1)} copy(bf16[8,4,512,64]{2,3,1,0:T(8,128)(2,1)S(1)} %all-to-all-done.1) | data formatting | bytes 4194304 | tf_op jit(solution)/shard_map/all_to_all | solution.py:250
  82.5 30.2 %shard_map.157 = bf16[2,3,512,64]{3,2,1,0:T(8,128)(2,1)} custom-call(s32[4]{0:T(128)} %get-tuple-element.38.lo_ref, s32[4]{0:T(128)} %get-tuple-element.37.hi_ref, bf16[2,3,512,64]{3,2,1,0:T(8,128)(2,1)} %maximum_bitcast_fusion.q_ref, bf16[8,4,512,64]{3,2,1,0:T(8,128)(2,1)} %copy.97.k_ref.v_ref, bf16[8,4,512,64]{3,2,1,0:T(8,128)(2,1)} %copy.97.k_ref.v_ref, ...), custom_call_target="tpu_custom_call" | custom-call | tf_op jit(solution)/shard_map/pallas_call | solution.py:186
  112.7 1.4 copy.100
  115.4 2.2 %collective-permute-done.2 = bf16[2,128,1536]{2,1,0:T(8,128)(2,1)S(1)} collective-permute-done((bf16[2,128,1536]{2,1,0:T(8,128)(2,1)S(1)}, bf16[2,128,1536]{2,1,0:T(8,128)(2,1)S(1)}, u32[]{:S(2)}, u32[]{:S(2)}) %collective-permute-start.2) | collective-permute-done | bytes 786464 | tf_op jit(solution)/shard_map/ppermute | solution.py:105
  119.8 10.6 %collective-permute-done.3 = bf16[128,1536]{1,0:T(8,128)(2,1)S(1)} collective-permute-done((bf16[128,1536]{1,0:T(8,128)(2,1)S(1)}, bf16[128,1536]{1,0:T(8,128)(2,1)S(1)}, u32[]{:S(2)}, u32[]{:S(2)}) %collective-permute-start.3) | collective-permute-done | bytes 393248 | tf_op jit(solution)/shard_map/ppermute | solution.py:110
  130.3 1.4 multiply_reduce_fusion
  134.0 3.5 %all-to-all-start.2 = ((f32[4,128,40]{1,2,0:T(8,128)}), f32[4,128,40]{1,2,0:T(8,128)S(1)}, u32[]{:S(2)}, u32[]{:S(2)}) async-start(f32[4,128,40]{1,2,0:T(8,128)} %broadcast_in_dim.53), calls=%async_computation.2 | async-start | bytes 163840 | tf_op jit(solution)/shard_map/all_to_all | solution.py:55
  137.6 5.9 %collective-permute-done.4 = bf16[128,1536]{1,0:T(8,128)(2,1)S(1)} collective-permute-done((bf16[128,1536]{1,0:T(8,128)(2,1)S(1)}, bf16[128,1536]{1,0:T(8,128)(2,1)S(1)}, u32[]{:S(2)}, u32[]{:S(2)}) %collective-permute-start.4) | collective-permute-done | bytes 393248 | tf_op jit(solution)/shard_map/ppermute | solution.py:84
  144.7 1.3 collective-permute-done.5
  146.2 2.0 %gather_fusion.1 = bf16[2,2,128,1536]{3,2,1,0:T(8,128)(2,1)} fusion(bf16[2,2,128,1536]{3,2,0,1:T(8,128)(2,1)S(1)} %maximum_select_fusion.1, s32[1024]{0:T(1024)} %pad_clamp_fusion), kind=kCustom, calls=%fused_computation.1 | custom fusion | bytes 3145736 | tf_op jit(solution)/shard_map/jit(_take)/gather | solution.py:89
  148.2 17.3 %fusion.4 = f32[10,192,1024]{2,1,0:T(8,128)} fusion(bf16[10,1536,1024]{2,1,0:T(8,128)(2,1)} %param.24, bf16[512,1536,1]{1,0,2:T(8,128)(2,1)} %bitcast.134, s32[10,512]{1,0:T(8,128)S(1)} %copy.105, pred[10,512]{1,0:T(8,128)(4,1)S(1)} %get-tuple-element.21), kind=kOutput, calls=%fused_computation.6 | convolution fusion | flops 9064611840 | bytes 40920064 | tf_op jit(solution)/shard_map/esd,edf->esf/dot_general | solution.py:298
  165.5 14.5 %fusion.17 = bf16[512,1536]{1,0:T(8,128)(2,1)S(1)} fusion(bf16[10,512,1536]{2,1,0:T(8,128)(2,1)} %param.25, f32[10,192,1024]{2,1,0:T(8,128)} %fusion.4, bf16[10,512]{1,0:T(8,128)(2,1)S(1)} %dynamic-slice_bitcast_fusion, s32[10,512]{1,0:T(8,128)S(1)} %copy.105, pred[10,512]{1,0:T(8,128)(4,1)S(1)} %get-tuple-element.21), kind=kOutput, calls=%fused_computation.16 | convolution fusion | flops 6052380672 | bytes 25201664 | tf_op jit(solution)/shard_map/esr,esd->rd/dot_general | solution.py:306
  184.8 2.9 %gather_fusion.2 = bf16[12,2,2,64,64]{4,3,2,1,0:T(8,128)(2,1)S(1)} fusion(bf16[8,2,2,8,64,64]{5,4,3,2,1,0:T(8,128)(2,1)} %bitcast.123, s32[12]{0:T(128)S(1)} %fusion.51), kind=kCustom, calls=%fused_computation.2 | custom fusion | bytes 786528 | tf_op jit(solution)/shard_map/gather | solution.py:264
  188.8 6.3 %collective-permute-done.7 = bf16[128,1536]{1,0:T(8,128)(2,1)S(1)} collective-permute-done((bf16[128,1536]{1,0:T(8,128)(2,1)S(1)}, bf16[128,1536]{1,0:T(8,128)(2,1)S(1)}, u32[]{:S(2)}, u32[]{:S(2)}) %collective-permute-start.7) | collective-permute-done | bytes 393248 | tf_op jit(solution)/shard_map/ppermute | solution.py:110
  (100 shorter events, 21.9 us)
Async XLA Ops:
  0.6 113.5 %copy-start = (bf16[384,1536]{1,0:T(8,128)(2,1)S(1)}, bf16[384,1536]{1,0:T(8,128)(2,1)}, u32[]{:S(2)}) copy-start(bf16[384,1536]{1,0:T(8,128)(2,1)} %param.23) | copy-start | bytes 3538948
  3.1 11.0 %collective-permute-start = (bf16[128,1536]{1,0:T(8,128)(2,1)S(1)}, bf16[128,1536]{1,0:T(8,128)(2,1)S(1)}, u32[]{:S(2)}, u32[]{:S(2)}) collective-permute-start(bf16[128,1536]{1,0:T(8,128)(2,1)S(1)} %fusion.40), channel_id=1, source_target_pairs={{0,2},{1,3},{2,0},{3,1},{4,6},{5,7},{6,4},{7,5},{8,10},{9,11},{10,... | collective-permute-start | bytes 1179656 | tf_op jit(solution)/shard_map/ppermute | solution.py:84
  5.9 10.0 %all-to-all-start = ((s32[32,1,128]{2,1,0:T(1,128)}), s32[32,1,128]{2,1,0:T(1,128)S(1)}, u32[]{:S(2)}, u32[]{:S(2)}) async-start(s32[32,1,128]{2,1,0:T(1,128)} %broadcast_in_dim.43), calls=%async_computation | async-start | bytes 32768 | tf_op jit(solution)/shard_map/all_to_all | solution.py:55
  14.2 4.2 %collective-permute-start.1 = (bf16[2,128,1536]{2,1,0:T(8,128)(2,1)S(1)}, bf16[2,128,1536]{2,1,0:T(8,128)(2,1)}, u32[]{:S(2)}, u32[]{:S(2)}) collective-permute-start(bf16[2,128,1536]{2,1,0:T(8,128)(2,1)S(1)} %get-tuple-element.32), channel_id=1, source_target_pairs={{0,1},{1,0},{2,3},{3,2},{4,5},{5,4},{6,7},{7,6},{8,9},{9,8},{10,11... | collective-permute-start | bytes 2359304 | tf_op jit(solution)/shard_map/ppermute | solution.py:86
  19.9 2.1 %copy-start.15 = (bf16[1536,128]{1,0:T(8,128)(2,1)S(1)}, bf16[1536,128]{1,0:T(8,128)(2,1)}, u32[]{:S(2)}) copy-start(bf16[1536,128]{1,0:T(8,128)(2,1)} %param.22) | copy-start | bytes 1179652
  19.9 2.1 %copy-start.16 = (bf16[1536,128]{1,0:T(8,128)(2,1)S(1)}, bf16[1536,128]{1,0:T(8,128)(2,1)}, u32[]{:S(2)}) copy-start(bf16[1536,128]{1,0:T(8,128)(2,1)} %param.21) | copy-start | bytes 1179652
  25.1 1.1 copy-start.7
  25.1 1.3 copy-start.9
  25.2 1.3 copy-start.10
  28.2 51.2 %all-to-all-start.1 = ((bf16[8,4,512,64]{2,3,1,0:T(8,128)(2,1)}), bf16[8,4,512,64]{2,3,1,0:T(8,128)(2,1)S(1)}, u32[]{:S(2)}, u32[]{:S(2)}) async-start(bf16[8,4,512,64]{2,3,1,0:T(8,128)(2,1)} %broadcast_in_dim.49), calls=%async_computation.1 | async-start | bytes 4194304 | tf_op jit(solution)/shard_map/all_to_all | solution.py:250
  115.2 2.4 %collective-permute-start.2 = (bf16[2,128,1536]{2,1,0:T(8,128)(2,1)S(1)}, bf16[2,128,1536]{2,1,0:T(8,128)(2,1)S(1)}, u32[]{:S(2)}, u32[]{:S(2)}) collective-permute-start(bf16[2,128,1536]{2,1,0:T(8,128)(2,1)S(1)} %select_bitcast_fusion.1), channel_id=1, source_target_pairs={{0,1},{1,0},{2,3},{3,2},{4,5},{5,4},{6,7},{7,6},{8,9},{9,8},{10,11... | collective-permute-start | bytes 2359304 | tf_op jit(solution)/shard_map/ppermute | solution.py:105
  115.3 15.0 %copy-start.4 = (bf16[128,1536]{1,0:T(8,128)(2,1)S(1)}, bf16[128,1536]{1,0:T(8,128)(2,1)}, u32[]{:S(2)}) copy-start(bf16[128,1536]{1,0:T(8,128)(2,1)} %param.14) | copy-start | bytes 1179652
  117.9 1.2 copy-start.2
  119.0 12.7 %copy-start.11 = (f32[1536]{0:T(1024)S(1)}, f32[1536]{0:T(1024)}, u32[]{:S(2)}) copy-start(f32[1536]{0:T(1024)} %param.19) | copy-start | bytes 18436
  119.1 12.7 %copy-start.3 = (f32[2,128,1536]{2,1,0:T(8,128)S(1)}, f32[2,128,1536]{2,1,0:T(8,128)}, u32[]{:S(2)}) copy-start(f32[2,128,1536]{2,1,0:T(8,128)} %copy-done.2) | copy-start | bytes 4718596
  119.1 11.2 %collective-permute-start.3 = (bf16[128,1536]{1,0:T(8,128)(2,1)S(1)}, bf16[128,1536]{1,0:T(8,128)(2,1)S(1)}, u32[]{:S(2)}, u32[]{:S(2)}) collective-permute-start(bf16[128,1536]{1,0:T(8,128)(2,1)S(1)} %fusion.42), channel_id=1, source_target_pairs={{0,2},{1,3},{2,0},{3,1},{4,6},{5,7},{6,4},{7,5},{8,10},{9,11},{10,... | collective-permute-start | bytes 1179656 | tf_op jit(solution)/shard_map/ppermute | solution.py:110
  131.7 1.6 copy-start.12
  131.7 1.6 copy-start.13
  132.7 10.8 %collective-permute-start.4 = (bf16[128,1536]{1,0:T(8,128)(2,1)S(1)}, bf16[128,1536]{1,0:T(8,128)(2,1)S(1)}, u32[]{:S(2)}, u32[]{:S(2)}) collective-permute-start(bf16[128,1536]{1,0:T(8,128)(2,1)S(1)} %get-tuple-element.25), channel_id=1, source_target_pairs={{0,2},{1,3},{2,0},{3,1},{4,6},{5,7},{6,4},{7,5},{8,10},{9,11},{10,... | collective-permute-start | bytes 1179656 | tf_op jit(solution)/shard_map/ppermute | solution.py:84
  134.0 9.9 %all-to-all-start.2 = ((f32[4,128,40]{1,2,0:T(8,128)}), f32[4,128,40]{1,2,0:T(8,128)S(1)}, u32[]{:S(2)}, u32[]{:S(2)}) async-start(f32[4,128,40]{1,2,0:T(8,128)} %broadcast_in_dim.53), calls=%async_computation.2 | async-start | bytes 163840 | tf_op jit(solution)/shard_map/all_to_all | solution.py:55
  143.6 2.4 %collective-permute-start.5 = (bf16[2,128,1536]{2,1,0:T(8,128)(2,1)S(1)}, bf16[2,128,1536]{2,1,0:T(8,128)(2,1)S(1)}, u32[]{:S(2)}, u32[]{:S(2)}) collective-permute-start(bf16[2,128,1536]{2,1,0:T(8,128)(2,1)S(1)} %get-tuple-element.30), channel_id=1, source_target_pairs={{0,1},{1,0},{2,3},{3,2},{4,5},{5,4},{6,7},{7,6},{8,9},{9,8},{10,11... | collective-permute-start | bytes 2359304 | tf_op jit(solution)/shard_map/ppermute | solution.py:86
  180.0 0.7 copy-start.14
  180.1 2.4 %collective-permute-start.6 = (bf16[2,128,1536]{2,1,0:T(8,128)(2,1)S(1)}, bf16[2,128,1536]{2,1,0:T(8,128)(2,1)S(1)}, u32[]{:S(2)}, u32[]{:S(2)}) collective-permute-start(bf16[2,128,1536]{2,1,0:T(8,128)(2,1)S(1)} %select_bitcast_fusion), channel_id=1, source_target_pairs={{0,1},{1,0},{2,3},{3,2},{4,5},{5,4},{6,7},{7,6},{8,9},{9,8},{10,11... | collective-permute-start | bytes 2359304 | tf_op jit(solution)/shard_map/ppermute | solution.py:105
  182.7 1.2 copy-start.5
  183.9 3.8 %copy-start.8 = (bf16[12,2,2,64,64]{4,3,2,1,0:T(8,128)(2,1)S(1)}, bf16[12,2,2,64,64]{4,3,2,1,0:T(8,128)(2,1)}, u32[]{:S(2)}) copy-start(bf16[12,2,2,64,64]{4,3,2,1,0:T(8,128)(2,1)} %param.26) | copy-start | bytes 1179652
  183.9 11.2 %collective-permute-start.7 = (bf16[128,1536]{1,0:T(8,128)(2,1)S(1)}, bf16[128,1536]{1,0:T(8,128)(2,1)S(1)}, u32[]{:S(2)}, u32[]{:S(2)}) collective-permute-start(bf16[128,1536]{1,0:T(8,128)(2,1)S(1)} %fusion.43), channel_id=1, source_target_pairs={{0,2},{1,3},{2,0},{3,1},{4,6},{5,7},{6,4},{7,5},{8,10},{9,11},{10,... | collective-permute-start | bytes 1179656 | tf_op jit(solution)/shard_map/ppermute | solution.py:110
  187.7 7.5 %copy-start.6 = (f32[2,128,1536]{2,1,0:T(8,128)S(1)}, f32[2,128,1536]{2,1,0:T(8,128)}, u32[]{:S(2)}) copy-start(f32[2,128,1536]{2,1,0:T(8,128)} %copy-done.5) | copy-start | bytes 4718596
  187.7 8.3 %copy-start.1 = (bf16[384,1536]{1,0:T(8,128)(2,1)S(1)}, bf16[384,1536]{1,0:T(8,128)(2,1)}, u32[]{:S(2)}) copy-start(bf16[384,1536]{1,0:T(8,128)(2,1)} %param.23) | copy-start | bytes 3538948

commit v5 on v4

--- a/solution.py
+++ b/solution.py
@@ -265,9 +265,11 @@
         0, 2, 1, 3, 4
     )
     new_cache = jnp.where(hit[:, None, None, None, None], picked, paged_key_value_cache)
-    head_out = head_out.transpose(2, 0, 1, 3).reshape(group_len, query_width)
+    out_weight = w_out_attn.reshape(kv_heads, heads_ratio, HEAD_SIZE, w_out_attn.shape[1])
     attention = scatter_sum_ep(
-        jnp.dot(head_out, w_out_attn, preferred_element_type=jnp.float32).astype(jnp.bfloat16)
+        jnp.einsum(
+            "grtd,grdo->to", head_out, out_weight, preferred_element_type=jnp.float32
+        ).astype(jnp.bfloat16)
     )
     attn_out = attention.astype(jnp.bfloat16)
     moe_in = rms_scale(tokens.astype(jnp.float32) + residual_scale * attention, norm2_gain).astype(

time: 199 us -> 201 us (1.010)
  the two profiles are of different devices: /device:TPU:12 before, /device:TPU:28 now
where the time goes in v5:
time: 201 us
  waiting for transfers between devices  61.3 us (30%)
  matrix products  37 us (18%)
  Pallas kernels  34.1 us (17%)
  local copies, waits for them, and re-layouts  27.7 us (14%)
  other arithmetic  19.8 us (10%)
  starting transfers between devices  19.5 us (10%)
    pallas_call x1, Pallas kernels, flash_attention(): pl.pallas_call(flash_body, grid_spec=grid_spec, out_shape=jax.ShapeDtypeS...  34.1 us
    all_to_all x1, waiting for transfers between devices, body(): lax.all_to_all(jnp.broadcast_to(kv_local[None], (req_count,) + kv_local.s...  31.4 us
    dot_general x1, matrix products, body(): jnp.einsum('esd,edf->esf', arrived, w_in, preferred_element_type=jnp.floa...  17.3 us
    ppermute x2, waiting for transfers between devices, scatter_sum_ep(): lax.ppermute(piece.astype(jnp.bfloat16), 'ep', chip_pairs(count, shift))  16.9 us
    dot_general x1, matrix products, body(): jnp.einsum('esr,esd->rd', combine.astype(jnp.bfloat16), result, preferred...  14.5 us
    all_to_all x2, starting transfers between devices, gather_rows(): got = lax.all_to_all(spread, axis_name, 0, 0, tiled=True)  8.39 us
    ppermute x2, waiting for transfers between devices, gather_ep(): side.append(lax.ppermute(x, 'ep', chip_pairs(count, shift)))  8.1 us
    all_to_all x1, starting transfers between devices, body(): lax.all_to_all(jnp.broadcast_to(kv_local[None], (req_count,) + kv_local.s...  7.26 us
  transfers between devices with their start and end apart: 11, of which 9 were waited for; matrix products, arithmetic and copies ran while one was open for 13% of the time, Pallas kernels for 0%

profile of v5, /device:TPU:28, one launch (start us, length us, event | category | flops | bytes accessed | tf_op | source)
XLA Modules:
  0.0 200.6 jit_solution(9908466703365967537)
XLA Ops:
  0.6 1.3 fusion.39
  1.9 1.2 fusion.41
  3.1 1.6 collective-permute-start
  4.6 1.3 broadcast_in_dim.43
  5.9 4.9 %all-to-all-start = ((s32[32,1,128]{2,1,0:T(1,128)}), s32[32,1,128]{2,1,0:T(1,128)S(1)}, u32[]{:S(2)}, u32[]{:S(2)}) async-start(s32[32,1,128]{2,1,0:T(1,128)} %broadcast_in_dim.43), calls=%async_computation | async-start | bytes 32768 | tf_op jit(solution)/shard_map/all_to_all | solution.py:55
  12.0 2.2 %collective-permute-done = bf16[128,1536]{1,0:T(8,128)(2,1)S(1)} collective-permute-done((bf16[128,1536]{1,0:T(8,128)(2,1)S(1)}, bf16[128,1536]{1,0:T(8,128)(2,1)S(1)}, u32[]{:S(2)}, u32[]{:S(2)}) %collective-permute-start) | collective-permute-done | bytes 393248 | tf_op jit(solution)/shard_map/ppermute | solution.py:84
  15.1 1.6 multiply_cosine_fusion
  16.7 1.6 maximum_select_fusion
  18.4 2.1 %gather_fusion = bf16[2,2,128,1536]{3,2,1,0:T(8,128)(2,1)} fusion(bf16[2,2,128,1536]{3,2,0,1:T(8,128)(2,1)S(1)} %maximum_select_fusion, s32[1024]{0:T(1024)} %pad_clamp_fusion), kind=kCustom, calls=%fused_computation | custom fusion | bytes 3145736 | tf_op jit(solution)/shard_map/jit(_take)/gather | solution.py:89
  20.4 3.1 %fusion.23 = f32[512,640]{1,0:T(8,128)S(1)} fusion(bf16[512,1536]{1,0:T(8,128)(2,1)} %bitcast.139, bf16[1536,128]{1,0:T(8,128)(2,1)S(1)} %copy-done.14, bf16[1536,128]{1,0:T(8,128)(2,1)S(1)} %copy-done.15, bf16[1536,384]{1,0:T(8,128)(2,1)} %param.20), kind=kOutput, calls=%fused_computation.18 | convolution fusion | flops 1012531200 | bytes 4849664 | tf_op jit(solution)/shard_map/dot_general | solution.py:221
  25.0 1.6 broadcast_in_dim.49
  26.6 7.3 %all-to-all-start.1 = ((bf16[8,4,512,64]{2,3,1,0:T(8,128)(2,1)}), bf16[8,4,512,64]{2,3,1,0:T(8,128)(2,1)S(1)}, u32[]{:S(2)}, u32[]{:S(2)}) async-start(bf16[8,4,512,64]{2,3,1,0:T(8,128)(2,1)} %broadcast_in_dim.49), calls=%async_computation.1 | async-start | bytes 4194304 | tf_op jit(solution)/shard_map/all_to_all | solution.py:250
  36.4 2.1 %slice.79 = f32[512,384]{1,0:T(8,128)} slice(f32[512,640]{1,0:T(8,128)} %copy-done.6), slice={[0:512], [0:384]} | slice | bytes 1572864 | tf_op jit(solution)/shard_map/slice | solution.py:230
  38.4 2.3 %copy.93 = f32[512,384]{0,1:T(8,128)} copy(f32[512,384]{1,0:T(8,128)} %slice.79) | data formatting | bytes 1572864 | tf_op jit(solution)/shard_map/slice | solution.py:230
  40.7 1.9 subtract_convert_fusion
  42.7 2.1 %copy.94 = bf16[512,6,32]{2,0,1:T(8,128)(2,1)} copy(bf16[512,6,32]{0,2,1:T(8,128)(2,1)} %get-tuple-element.27) | data formatting | bytes 393216 | tf_op jit(solution)/shard_map/convert.8
  45.9 2.7 %maximum_bitcast_fusion.q_ref = bf16[2,3,512,64]{3,2,1,0:T(8,128)(2,1)} fusion(bf16[512,2,3,32]{3,0,2,1:T(8,128)(2,1)} %bitcast.136, bf16[512,2,3,32]{3,0,2,1:T(8,128)(2,1)} %bitcast.135), kind=kLoop, calls=%fused_computation.46 | loop fusion | flops 786432 | bytes 786432 | tf_op jit(solution)/shard_map/transpose | solution.py:243
  48.6 31.4 %all-to-all-done.1 = bf16[8,4,512,64]{2,3,1,0:T(8,128)(2,1)S(1)} async-done(((bf16[8,4,512,64]{2,3,1,0:T(8,128)(2,1)}), bf16[8,4,512,64]{2,3,1,0:T(8,128)(2,1)S(1)}, u32[]{:S(2)}, u32[]{:S(2)}) %all-to-all-start.1) | async-done | bytes 2097184 | tf_op jit(solution)/shard_map/all_to_all | solution.py:250
  80.0 3.2 %copy.98.k_ref.v_ref = bf16[8,4,512,64]{3,2,1,0:T(8,128)(2,1)} copy(bf16[8,4,512,64]{2,3,1,0:T(8,128)(2,1)S(1)} %all-to-all-done.1) | data formatting | bytes 4194304 | tf_op jit(solution)/shard_map/all_to_all | solution.py:250
  83.2 34.1 %shard_map.157 = bf16[2,3,512,64]{3,2,1,0:T(8,128)(2,1)} custom-call(s32[4]{0:T(128)} %get-tuple-element.38.lo_ref, s32[4]{0:T(128)} %get-tuple-element.37.hi_ref, bf16[2,3,512,64]{3,2,1,0:T(8,128)(2,1)} %maximum_bitcast_fusion.q_ref, bf16[8,4,512,64]{3,2,1,0:T(8,128)(2,1)} %copy.98.k_ref.v_ref, bf16[8,4,512,64]{3,2,1,0:T(8,128)(2,1)} %copy.98.k_ref.v_ref, ...), custom_call_target="tpu_custom_call" | custom-call | tf_op jit(solution)/shard_map/pallas_call | solution.py:186
  117.4 2.2 %fusion.17 = bf16[512,1536]{1,0:T(8,128)(2,1)S(1)} fusion(bf16[2,3,512,64]{3,2,1,0:T(8,128)(2,1)} %shard_map.157, bf16[2,3,64,1536]{3,2,1,0:T(8,128)(2,1)S(1)} %bitcast.128), kind=kOutput, calls=%fused_computation.16 | convolution fusion | flops 604766208 | bytes 3145728 | tf_op jit(solution)/shard_map/grtd,grdo->to/dot_general | solution.py:270
  120.9 2.2 %collective-permute-done.2 = bf16[2,128,1536]{2,1,0:T(8,128)(2,1)S(1)} collective-permute-done((bf16[2,128,1536]{2,1,0:T(8,128)(2,1)S(1)}, bf16[2,128,1536]{2,1,0:T(8,128)(2,1)S(1)}, u32[]{:S(2)}, u32[]{:S(2)}) %collective-permute-start.2) | collective-permute-done | bytes 786464 | tf_op jit(solution)/shard_map/ppermute | solution.py:105
  123.1 1.7 convert_add_fusion.1
  125.5 10.6 %collective-permute-done.3 = bf16[128,1536]{1,0:T(8,128)(2,1)S(1)} collective-permute-done((bf16[128,1536]{1,0:T(8,128)(2,1)S(1)}, bf16[128,1536]{1,0:T(8,128)(2,1)S(1)}, u32[]{:S(2)}, u32[]{:S(2)}) %collective-permute-start.3) | collective-permute-done | bytes 393248 | tf_op jit(solution)/shard_map/ppermute | solution.py:110
  138.6 3.5 %all-to-all-start.2 = ((f32[4,128,40]{1,2,0:T(8,128)}), f32[4,128,40]{1,2,0:T(8,128)S(1)}, u32[]{:S(2)}, u32[]{:S(2)}) async-start(f32[4,128,40]{1,2,0:T(8,128)} %broadcast_in_dim.53), calls=%async_computation.2 | async-start | bytes 163840 | tf_op jit(solution)/shard_map/all_to_all | solution.py:55
  142.2 5.9 %collective-permute-done.4 = bf16[128,1536]{1,0:T(8,128)(2,1)S(1)} collective-permute-done((bf16[128,1536]{1,0:T(8,128)(2,1)S(1)}, bf16[128,1536]{1,0:T(8,128)(2,1)S(1)}, u32[]{:S(2)}, u32[]{:S(2)}) %collective-permute-start.4) | collective-permute-done | bytes 393248 | tf_op jit(solution)/shard_map/ppermute | solution.py:84
  149.3 1.3 collective-permute-done.5
  150.8 2.0 gather_fusion.1
  152.8 17.3 %fusion.4 = f32[10,192,1024]{2,1,0:T(8,128)} fusion(bf16[10,1536,1024]{2,1,0:T(8,128)(2,1)} %param.24, bf16[512,1536,1]{1,0,2:T(8,128)(2,1)} %bitcast.138, s32[10,512]{1,0:T(8,128)S(1)} %copy.106, pred[10,512]{1,0:T(8,128)(4,1)S(1)} %get-tuple-element.21), kind=kOutput, calls=%fused_computation.6 | convolution fusion | flops 9064611840 | bytes 40920064 | tf_op jit(solution)/shard_map/esd,edf->esf/dot_general | solution.py:300
  170.1 14.5 %fusion.18 = bf16[512,1536]{1,0:T(8,128)(2,1)S(1)} fusion(bf16[10,512,1536]{2,1,0:T(8,128)(2,1)} %param.25, f32[10,192,1024]{2,1,0:T(8,128)} %fusion.4, bf16[10,512]{1,0:T(8,128)(2,1)S(1)} %dynamic-slice_bitcast_fusion, s32[10,512]{1,0:T(8,128)S(1)} %copy.106, pred[10,512]{1,0:T(8,128)(4,1)S(1)} %get-tuple-element.21), kind=kOutput, calls=%fused_computation.17 | convolution fusion | flops 6052380672 | bytes 25201664 | tf_op jit(solution)/shard_map/esr,esd->rd/dot_general | solution.py:308
  189.4 2.9 %gather_fusion.2 = bf16[12,2,2,64,64]{4,3,2,1,0:T(8,128)(2,1)S(1)} fusion(bf16[8,2,2,8,64,64]{5,4,3,2,1,0:T(8,128)(2,1)} %bitcast.129, s32[12]{0:T(128)S(1)} %fusion.52), kind=kCustom, calls=%fused_computation.2 | custom fusion | bytes 786528 | tf_op jit(solution)/shard_map/gather | solution.py:264
  193.4 6.3 %collective-permute-done.7 = bf16[128,1536]{1,0:T(8,128)(2,1)S(1)} collective-permute-done((bf16[128,1536]{1,0:T(8,128)(2,1)S(1)}, bf16[128,1536]{1,0:T(8,128)(2,1)S(1)}, u32[]{:S(2)}, u32[]{:S(2)}) %collective-permute-start.7) | collective-permute-done | bytes 393248 | tf_op jit(solution)/shard_map/ppermute | solution.py:110
  (97 shorter events, 19.8 us)
Async XLA Ops:
  0.6 116.8 %copy-start = (bf16[384,1536]{1,0:T(8,128)(2,1)S(1)}, bf16[384,1536]{1,0:T(8,128)(2,1)}, u32[]{:S(2)}) copy-start(bf16[384,1536]{1,0:T(8,128)(2,1)} %param.23) | copy-start | bytes 3538948
  3.1 11.1 %collective-permute-start = (bf16[128,1536]{1,0:T(8,128)(2,1)S(1)}, bf16[128,1536]{1,0:T(8,128)(2,1)S(1)}, u32[]{:S(2)}, u32[]{:S(2)}) collective-permute-start(bf16[128,1536]{1,0:T(8,128)(2,1)S(1)} %fusion.41), channel_id=1, source_target_pairs={{0,2},{1,3},{2,0},{3,1},{4,6},{5,7},{6,4},{7,5},{8,10},{9,11},{10,... | collective-permute-start | bytes 1179656 | tf_op jit(solution)/shard_map/ppermute | solution.py:84
  5.9 8.4 %all-to-all-start = ((s32[32,1,128]{2,1,0:T(1,128)}), s32[32,1,128]{2,1,0:T(1,128)S(1)}, u32[]{:S(2)}, u32[]{:S(2)}) async-start(s32[32,1,128]{2,1,0:T(1,128)} %broadcast_in_dim.43), calls=%async_computation | async-start | bytes 32768 | tf_op jit(solution)/shard_map/all_to_all | solution.py:55
  14.3 2.5 %collective-permute-start.1 = (bf16[2,128,1536]{2,1,0:T(8,128)(2,1)S(1)}, bf16[2,128,1536]{2,1,0:T(8,128)(2,1)}, u32[]{:S(2)}, u32[]{:S(2)}) collective-permute-start(bf16[2,128,1536]{2,1,0:T(8,128)(2,1)S(1)} %get-tuple-element.32), channel_id=1, source_target_pairs={{0,1},{1,0},{2,3},{3,2},{4,5},{5,4},{6,7},{7,6},{8,9},{9,8},{10,11... | collective-permute-start | bytes 2359304 | tf_op jit(solution)/shard_map/ppermute | solution.py:86
  18.4 2.1 %copy-start.14 = (bf16[1536,128]{1,0:T(8,128)(2,1)S(1)}, bf16[1536,128]{1,0:T(8,128)(2,1)}, u32[]{:S(2)}) copy-start(bf16[1536,128]{1,0:T(8,128)(2,1)} %param.22) | copy-start | bytes 1179652
  18.4 2.1 %copy-start.15 = (bf16[1536,128]{1,0:T(8,128)(2,1)S(1)}, bf16[1536,128]{1,0:T(8,128)(2,1)}, u32[]{:S(2)}) copy-start(bf16[1536,128]{1,0:T(8,128)(2,1)} %param.21) | copy-start | bytes 1179652
  23.6 1.1 copy-start.6
  23.6 1.3 copy-start.8
  23.6 1.3 copy-start.9
  26.6 53.4 %all-to-all-start.1 = ((bf16[8,4,512,64]{2,3,1,0:T(8,128)(2,1)}), bf16[8,4,512,64]{2,3,1,0:T(8,128)(2,1)S(1)}, u32[]{:S(2)}, u32[]{:S(2)}) async-start(bf16[8,4,512,64]{2,3,1,0:T(8,128)(2,1)} %broadcast_in_dim.49), calls=%async_computation.1 | async-start | bytes 4194304 | tf_op jit(solution)/shard_map/all_to_all | solution.py:250
  119.5 1.2 copy-start.2
  120.8 2.4 %collective-permute-start.2 = (bf16[2,128,1536]{2,1,0:T(8,128)(2,1)S(1)}, bf16[2,128,1536]{2,1,0:T(8,128)(2,1)S(1)}, u32[]{:S(2)}, u32[]{:S(2)}) collective-permute-start(bf16[2,128,1536]{2,1,0:T(8,128)(2,1)S(1)} %select_bitcast_fusion.1), channel_id=1, source_target_pairs={{0,1},{1,0},{2,3},{3,2},{4,5},{5,4},{6,7},{7,6},{8,9},{9,8},{10,11... | collective-permute-start | bytes 2359304 | tf_op jit(solution)/shard_map/ppermute | solution.py:105
  120.9 15.2 %copy-start.3 = (bf16[128,1536]{1,0:T(8,128)(2,1)S(1)}, bf16[128,1536]{1,0:T(8,128)(2,1)}, u32[]{:S(2)}) copy-start(bf16[128,1536]{1,0:T(8,128)(2,1)} %param.14) | copy-start | bytes 1179652
  124.8 11.6 %copy-start.10 = (f32[1536]{0:T(1024)S(1)}, f32[1536]{0:T(1024)}, u32[]{:S(2)}) copy-start(f32[1536]{0:T(1024)} %param.19) | copy-start | bytes 18436
  124.9 11.2 %collective-permute-start.3 = (bf16[128,1536]{1,0:T(8,128)(2,1)S(1)}, bf16[128,1536]{1,0:T(8,128)(2,1)S(1)}, u32[]{:S(2)}, u32[]{:S(2)}) collective-permute-start(bf16[128,1536]{1,0:T(8,128)(2,1)S(1)} %fusion.43), channel_id=1, source_target_pairs={{0,2},{1,3},{2,0},{3,1},{4,6},{5,7},{6,4},{7,5},{8,10},{9,11},{10,... | collective-permute-start | bytes 1179656 | tf_op jit(solution)/shard_map/ppermute | solution.py:110
  136.4 1.6 copy-start.11
  136.4 1.6 copy-start.12
  137.4 10.8 %collective-permute-start.4 = (bf16[128,1536]{1,0:T(8,128)(2,1)S(1)}, bf16[128,1536]{1,0:T(8,128)(2,1)S(1)}, u32[]{:S(2)}, u32[]{:S(2)}) collective-permute-start(bf16[128,1536]{1,0:T(8,128)(2,1)S(1)} %get-tuple-element.25), channel_id=1, source_target_pairs={{0,2},{1,3},{2,0},{3,1},{4,6},{5,7},{6,4},{7,5},{8,10},{9,11},{10,... | collective-permute-start | bytes 1179656 | tf_op jit(solution)/shard_map/ppermute | solution.py:84
  138.6 9.9 %all-to-all-start.2 = ((f32[4,128,40]{1,2,0:T(8,128)}), f32[4,128,40]{1,2,0:T(8,128)S(1)}, u32[]{:S(2)}, u32[]{:S(2)}) async-start(f32[4,128,40]{1,2,0:T(8,128)} %broadcast_in_dim.53), calls=%async_computation.2 | async-start | bytes 163840 | tf_op jit(solution)/shard_map/all_to_all | solution.py:55
  148.2 2.4 %collective-permute-start.5 = (bf16[2,128,1536]{2,1,0:T(8,128)(2,1)S(1)}, bf16[2,128,1536]{2,1,0:T(8,128)(2,1)S(1)}, u32[]{:S(2)}, u32[]{:S(2)}) collective-permute-start(bf16[2,128,1536]{2,1,0:T(8,128)(2,1)S(1)} %get-tuple-element.30), channel_id=1, source_target_pairs={{0,1},{1,0},{2,3},{3,2},{4,5},{5,4},{6,7},{7,6},{8,9},{9,8},{10,11... | collective-permute-start | bytes 2359304 | tf_op jit(solution)/shard_map/ppermute | solution.py:86
  184.6 0.7 copy-start.13
  184.7 2.4 %collective-permute-start.6 = (bf16[2,128,1536]{2,1,0:T(8,128)(2,1)S(1)}, bf16[2,128,1536]{2,1,0:T(8,128)(2,1)S(1)}, u32[]{:S(2)}, u32[]{:S(2)}) collective-permute-start(bf16[2,128,1536]{2,1,0:T(8,128)(2,1)S(1)} %select_bitcast_fusion), channel_id=1, source_target_pairs={{0,1},{1,0},{2,3},{3,2},{4,5},{5,4},{6,7},{7,6},{8,9},{9,8},{10,11... | collective-permute-start | bytes 2359304 | tf_op jit(solution)/shard_map/ppermute | solution.py:105
  187.4 1.2 copy-start.4
  188.5 3.8 %copy-start.7 = (bf16[12,2,2,64,64]{4,3,2,1,0:T(8,128)(2,1)S(1)}, bf16[12,2,2,64,64]{4,3,2,1,0:T(8,128)(2,1)}, u32[]{:S(2)}) copy-start(bf16[12,2,2,64,64]{4,3,2,1,0:T(8,128)(2,1)} %param.26) | copy-start | bytes 1179652
  188.6 11.2 %collective-permute-start.7 = (bf16[128,1536]{1,0:T(8,128)(2,1)S(1)}, bf16[128,1536]{1,0:T(8,128)(2,1)S(1)}, u32[]{:S(2)}, u32[]{:S(2)}) collective-permute-start(bf16[128,1536]{1,0:T(8,128)(2,1)S(1)} %fusion.44), channel_id=1, source_target_pairs={{0,2},{1,3},{2,0},{3,1},{4,6},{5,7},{6,4},{7,5},{8,10},{9,11},{10,... | collective-permute-start | bytes 1179656 | tf_op jit(solution)/shard_map/ppermute | solution.py:110
  192.3 7.5 %copy-start.5 = (f32[2,128,1536]{2,1,0:T(8,128)S(1)}, f32[2,128,1536]{2,1,0:T(8,128)}, u32[]{:S(2)}) copy-start(f32[2,128,1536]{2,1,0:T(8,128)} %copy-done.4) | copy-start | bytes 4718596
  192.3 8.3 %copy-start.1 = (bf16[384,1536]{1,0:T(8,128)(2,1)S(1)}, bf16[384,1536]{1,0:T(8,128)(2,1)}, u32[]{:S(2)}) copy-start(bf16[384,1536]{1,0:T(8,128)(2,1)} %param.23) | copy-start | bytes 3538948

commit v6 on v5

--- a/solution.py
+++ b/solution.py
@@ -123,7 +123,7 @@
     q_tile = q_ref.shape[2]
     head_dim = q_ref.shape[3]
     q = q_ref[0].reshape(ratio * q_tile, head_dim)
-    per_group = k_ref.shape[2] // K_TILE
+    per_group = k_ref.shape[3] // K_TILE
     tok = tok_ref[...]
     begin = begin_ref[...]
 
@@ -132,10 +132,10 @@
         k0 = kb * K_TILE
         grp = kb // per_group
         off = pl.multiple_of((kb % per_group) * K_TILE, K_TILE)
-        k_blk = k_ref[grp, 0, pl.ds(off, K_TILE), :]
-        v_blk = v_ref[grp, 0, pl.ds(off, K_TILE), :]
+        k_blk = k_ref[grp, 0, :, pl.ds(off, K_TILE)]
+        v_blk = v_ref[grp, 0, :, pl.ds(off, K_TILE)]
         s = lax.dot_general(
-            q, k_blk, (((1,), (1,)), ((), ())), preferred_element_type=jnp.float32
+            q, k_blk, (((1,), (0,)), ((), ())), preferred_element_type=jnp.float32
         )
         s = (s * score_scale).reshape(ratio, q_tile, K_TILE)
         key_at = k0 + lax.broadcasted_iota(jnp.int32, (q_tile, K_TILE), 1)
@@ -148,7 +148,7 @@
         pv = lax.dot_general(
             p.reshape(ratio * q_tile, K_TILE).astype(jnp.bfloat16),
             v_blk,
-            (((1,), (0,)), ((), ())),
+            (((1,), (1,)), ((), ())),
             preferred_element_type=jnp.float32,
         )
         acc_new = alpha * acc_old + pv.reshape(ratio, q_tile, head_dim)
@@ -165,7 +165,7 @@
 
 def flash_attention(query_grouped, kv_all, q_index, q_begin):
     kv_heads, ratio, group_len, head_dim = query_grouped.shape
-    n_grp, _, grp_len, _ = kv_all.shape
+    n_grp, _, _, grp_len = kv_all.shape
     n_q = group_len // Q_TILE
     lo = jnp.min(q_begin.reshape(n_q, Q_TILE), axis=1) // K_TILE
     hi = jnp.max(q_index.reshape(n_q, Q_TILE), axis=1) // K_TILE
@@ -174,9 +174,9 @@
         grid=(kv_heads, n_q),
         in_specs=[
             pl.BlockSpec((1, ratio, Q_TILE, head_dim), lambda g, qb, lo, hi: (g, 0, qb, 0)),
-            pl.BlockSpec((n_grp, 1, grp_len, head_dim), lambda g, qb, lo, hi: (0, g, 0, 0)),
+            pl.BlockSpec((n_grp, 1, head_dim, grp_len), lambda g, qb, lo, hi: (0, g, 0, 0)),
             pl.BlockSpec(
-                (n_grp, 1, grp_len, head_dim), lambda g, qb, lo, hi: (0, kv_heads + g, 0, 0)
+                (n_grp, 1, head_dim, grp_len), lambda g, qb, lo, hi: (0, kv_heads + g, 0, 0)
             ),
             pl.BlockSpec((Q_TILE, 1), lambda g, qb, lo, hi: (qb, 0)),
             pl.BlockSpec((Q_TILE, 1), lambda g, qb, lo, hi: (qb, 0)),
@@ -247,6 +247,7 @@
         [key_rows.transpose(1, 0, 2), value_rows.transpose(1, 0, 2)], axis=0
     )
     req_count = lax.axis_size("req")
+    kv_local = kv_local.swapaxes(1, 2)
     kv_all = lax.all_to_all(
         jnp.broadcast_to(kv_local[None], (req_count,) + kv_local.shape), "req", 0, 0, tiled=True
     )
@@ -260,9 +261,9 @@
     match = local_pages[:, None] == page_table[None, :]
     hit = jnp.any(match, axis=1)
     block_of = jnp.argmax(match, axis=1).astype(jnp.int32)
-    kv_paged = kv_all.reshape(req_count, 2, kv_heads, group_pages, PAGE_TOKENS, HEAD_SIZE)
-    picked = kv_paged[block_of // group_pages, :, :, block_of % group_pages].transpose(
-        0, 2, 1, 3, 4
+    kv_paged = kv_all.reshape(req_count, 2, kv_heads, HEAD_SIZE, group_pages, PAGE_TOKENS)
+    picked = kv_paged[block_of // group_pages, :, :, :, block_of % group_pages].transpose(
+        0, 2, 1, 4, 3
     )
     new_cache = jnp.where(hit[:, None, None, None, None], picked, paged_key_value_cache)
     out_weight = w_out_attn.reshape(kv_heads, heads_ratio, HEAD_SIZE, w_out_attn.shape[1])

time: 201 us -> 214 us (1.065)
  the two profiles are of different devices: /device:TPU:28 before, /device:TPU:17 now
where the time goes in v6:
time: 214 us; the launch traced here: 213 us
  waiting for transfers between devices  48.3 us (23%)
  local copies, waits for them, and re-layouts  39.8 us (19%)
  Pallas kernels  37.5 us (18%)
  matrix products  37 us (17%)
  other arithmetic  24.8 us (12%)
  starting transfers between devices  24.6 us (11%)
    pallas_call x1, Pallas kernels, flash_attention(): pl.pallas_call(flash_body, grid_spec=grid_spec, out_shape=jax.ShapeDtypeS...  37.5 us
    all_to_all x1, waiting for transfers between devices, body(): lax.all_to_all(jnp.broadcast_to(kv_local[None], (req_count,) + kv_local.s...  30 us
    dot_general x1, matrix products, body(): jnp.einsum('esd,edf->esf', arrived, w_in, preferred_element_type=jnp.floa...  17.3 us
    dot_general x1, matrix products, body(): jnp.einsum('esr,esd->rd', combine.astype(jnp.bfloat16), result, preferred...  14.5 us
    all_to_all x2, starting transfers between devices, gather_rows(): got = lax.all_to_all(spread, axis_name, 0, 0, tiled=True)  10.3 us
    ppermute x2, waiting for transfers between devices, scatter_sum_ep(): lax.ppermute(piece.astype(jnp.bfloat16), 'ep', chip_pairs(count, shift))  10 us
    unnamed x42, local copies, waits for them, and re-layouts  9.4 us
    reshape x2, local copies, waits for them, and re-layouts, body(): kv_all.reshape(req_count, 2, kv_heads, HEAD_SIZE, group_pages, PAGE_TOKENS)  8.96 us
  transfers between devices with their start and end apart: 11, of which 7 were waited for; matrix products, arithmetic and copies ran while one was open for 19% of the time, Pallas kernels for 0%

profile of v6, /device:TPU:17, one launch (start us, length us, event | category | flops | bytes accessed | tf_op | source)
XLA Modules:
  0.0 213.0 jit_solution(16557976326341930528)
XLA Ops:
  5.6 5.6 %all-to-all-start = ((s32[32,1,128]{2,1,0:T(1,128)}), s32[32,1,128]{2,1,0:T(1,128)S(1)}, u32[]{:S(2)}, u32[]{:S(2)}) async-start(s32[32,1,128]{2,1,0:T(1,128)} %broadcast_in_dim.43), calls=%async_computation | async-start | bytes 32768 | tf_op jit(solution)/shard_map/all_to_all | solution.py:55
  13.2 1.7 collective-permute-start.1
  16.6 1.6 multiply_cosine_fusion
  18.2 1.6 maximum_select_fusion
  19.9 2.1 gather_fusion
  21.9 3.1 %fusion.23 = f32[512,640]{1,0:T(8,128)S(1)} fusion(bf16[512,1536]{1,0:T(8,128)(2,1)} %bitcast.141, bf16[1536,128]{1,0:T(8,128)(2,1)S(1)} %copy-done.18, bf16[1536,128]{1,0:T(8,128)(2,1)S(1)} %copy-done.19, bf16[1536,384]{1,0:T(8,128)(2,1)} %param.20), kind=kOutput, calls=%fused_computation.18 | convolution fusion | flops 1012531200 | bytes 4849664 | tf_op jit(solution)/shard_map/dot_general | solution.py:221
  26.5 1.6 broadcast_in_dim.49
  28.1 5.7 %all-to-all-start.1 = ((bf16[8,4,64,512]{3,2,1,0:T(8,128)(2,1)}), bf16[8,4,64,512]{3,2,1,0:T(8,128)(2,1)S(1)}, u32[]{:S(2)}, u32[]{:S(2)}) async-start(bf16[8,4,64,512]{3,2,1,0:T(8,128)(2,1)} %broadcast_in_dim.49), calls=%async_computation.1 | async-start | bytes 4194304 | tf_op jit(solution)/shard_map/all_to_all | solution.py:251
  36.3 2.1 slice.79
  38.4 2.3 %copy.91 = f32[512,384]{0,1:T(8,128)} copy(f32[512,384]{1,0:T(8,128)} %slice.79) | data formatting | bytes 1572864 | tf_op jit(solution)/shard_map/slice | solution.py:230
  40.7 1.9 subtract_convert_fusion
  42.6 2.1 copy.92
  45.8 2.7 %maximum_bitcast_fusion.q_ref = bf16[2,3,512,64]{3,2,1,0:T(8,128)(2,1)} fusion(bf16[512,2,3,32]{3,0,2,1:T(8,128)(2,1)} %bitcast.138, bf16[512,2,3,32]{3,0,2,1:T(8,128)(2,1)} %bitcast.137), kind=kLoop, calls=%fused_computation.46 | loop fusion | flops 786432 | bytes 786432 | tf_op jit(solution)/shard_map/transpose | solution.py:243
  48.5 30.0 %all-to-all-done.1.k_ref.v_ref = bf16[8,4,64,512]{3,2,1,0:T(8,128)(2,1)S(1)} async-done(((bf16[8,4,64,512]{3,2,1,0:T(8,128)(2,1)}), bf16[8,4,64,512]{3,2,1,0:T(8,128)(2,1)S(1)}, u32[]{:S(2)}, u32[]{:S(2)}) %all-to-all-start.1) | async-done | bytes 2097184 | tf_op jit(solution)/shard_map/all_to_all | solution.py:251
  80.0 37.5 %shard_map.157 = bf16[2,3,512,64]{3,2,1,0:T(8,128)(2,1)} custom-call(s32[4]{0:T(128)} %get-tuple-element.38.lo_ref, s32[4]{0:T(128)} %get-tuple-element.37.hi_ref, bf16[2,3,512,64]{3,2,1,0:T(8,128)(2,1)} %maximum_bitcast_fusion.q_ref, bf16[8,4,64,512]{3,2,1,0:T(8,128)(2,1)} %copy-done.2, bf16[8,4,64,512]{3,2,1,0:T(8,128)(2,1)} %copy-done.2, ...), custom_call_target="tpu_custom_call" | custom-call | tf_op jit(solution)/shard_map/pallas_call | solution.py:186
  117.4 2.2 %fusion.17 = bf16[512,1536]{1,0:T(8,128)(2,1)S(1)} fusion(bf16[2,3,512,64]{3,2,1,0:T(8,128)(2,1)} %shard_map.157, bf16[2,3,64,1536]{3,2,1,0:T(8,128)(2,1)S(1)} %bitcast.131), kind=kOutput, calls=%fused_computation.16 | convolution fusion | flops 604766208 | bytes 3145728 | tf_op jit(solution)/shard_map/grtd,grdo->to/dot_general | solution.py:271
  122.4 1.9 collective-permute-done.2
  124.3 1.7 convert_add_fusion.1
  126.4 10.0 %collective-permute-done.3 = bf16[128,1536]{1,0:T(8,128)(2,1)S(1)} collective-permute-done((bf16[128,1536]{1,0:T(8,128)(2,1)S(1)}, bf16[128,1536]{1,0:T(8,128)(2,1)S(1)}, u32[]{:S(2)}, u32[]{:S(2)}) %collective-permute-start.3) | collective-permute-done | bytes 393248 | tf_op jit(solution)/shard_map/ppermute | solution.py:110
  138.6 4.7 %all-to-all-start.2 = ((f32[4,128,40]{1,2,0:T(8,128)}), f32[4,128,40]{1,2,0:T(8,128)S(1)}, u32[]{:S(2)}, u32[]{:S(2)}) async-start(f32[4,128,40]{1,2,0:T(8,128)} %broadcast_in_dim.53), calls=%async_computation.2 | async-start | bytes 163840 | tf_op jit(solution)/shard_map/all_to_all | solution.py:55
  143.5 3.6 %collective-permute-done.4 = bf16[128,1536]{1,0:T(8,128)(2,1)S(1)} collective-permute-done((bf16[128,1536]{1,0:T(8,128)(2,1)S(1)}, bf16[128,1536]{1,0:T(8,128)(2,1)S(1)}, u32[]{:S(2)}, u32[]{:S(2)}) %collective-permute-start.4) | collective-permute-done | bytes 393248 | tf_op jit(solution)/shard_map/ppermute | solution.py:84
  147.2 2.6 %collective-permute-start.5 = (bf16[2,128,1536]{2,1,0:T(8,128)(2,1)S(1)}, bf16[2,128,1536]{2,1,0:T(8,128)(2,1)S(1)}, u32[]{:S(2)}, u32[]{:S(2)}) collective-permute-start(bf16[2,128,1536]{2,1,0:T(8,128)(2,1)S(1)} %get-tuple-element.30), channel_id=1, source_target_pairs={{0,1},{1,0},{2,3},{3,2},{4,5},{5,4},{6,7},{7,6},{8,9},{9,8},{10,11... | collective-permute-start | bytes 2359304 | tf_op jit(solution)/shard_map/ppermute | solution.py:86
  152.0 1.9 gather_fusion.1
  153.9 17.3 %fusion.4 = f32[10,192,1024]{2,1,0:T(8,128)} fusion(bf16[10,1536,1024]{2,1,0:T(8,128)(2,1)} %param.24, bf16[512,1536,1]{1,0,2:T(8,128)(2,1)} %bitcast.140, s32[10,512]{1,0:T(8,128)S(1)} %copy.102, pred[10,512]{1,0:T(8,128)(4,1)S(1)} %get-tuple-element.21), kind=kOutput, calls=%fused_computation.6 | convolution fusion | flops 9064611840 | bytes 40920064 | tf_op jit(solution)/shard_map/esd,edf->esf/dot_general | solution.py:301
  171.2 14.5 %fusion.18 = bf16[512,1536]{1,0:T(8,128)(2,1)S(1)} fusion(bf16[10,512,1536]{2,1,0:T(8,128)(2,1)} %param.25, f32[10,192,1024]{2,1,0:T(8,128)} %fusion.4, bf16[10,512]{1,0:T(8,128)(2,1)S(1)} %dynamic-slice_bitcast_fusion, s32[10,512]{1,0:T(8,128)S(1)} %copy.102, pred[10,512]{1,0:T(8,128)(4,1)S(1)} %get-tuple-element.21), kind=kOutput, calls=%fused_computation.17 | convolution fusion | flops 6052380672 | bytes 25201664 | tf_op jit(solution)/shard_map/esr,esd->rd/dot_general | solution.py:309
  189.3 2.1 convert_add_fusion
  193.8 3.6 %reshape.241 = bf16[8,2,2,64,8,64]{5,4,3,2,1,0:T(8,128)(2,1)} reshape(bf16[8,4,64,512]{3,2,1,0:T(8,128)(2,1)S(1)} %copy-done.3) | data formatting | bytes 4194304 | tf_op jit(solution)/shard_map/reshape | solution.py:264
  197.4 5.3 %copy.105 = bf16[8,2,2,64,8,64]{5,3,4,2,1,0:T(8,128)(2,1)} copy(bf16[8,2,2,64,8,64]{5,4,3,2,1,0:T(8,128)(2,1)} %reshape.241) | data formatting | bytes 4194304 | tf_op jit(solution)/shard_map/reshape | solution.py:264
  202.8 3.8 %gather_fusion.2 = bf16[12,2,2,64,64]{4,3,2,1,0:T(8,128)(2,1)} fusion(bf16[8,2,2,64,8,64]{5,3,4,2,1,0:T(8,128)(2,1)} %copy.105, s32[12]{0:T(128)S(1)} %fusion.52), kind=kCustom, calls=%fused_computation.2 | custom fusion | bytes 786528 | tf_op jit(solution)/shard_map/gather | solution.py:265
  206.6 2.3 %bitcast_select_fusion = bf16[12,2,2,64,64]{3,4,1,2,0:T(8,128)(2,1)} fusion(bf16[12,2,2,64,64]{3,4,1,2,0:T(8,128)(2,1)S(1)} %copy-done.9, bf16[12,2,2,64,64]{4,3,2,1,0:T(8,128)(2,1)} %gather_fusion.2, pred[12]{0:T(512)(128)(4,1)S(1)} %compare_reduce_fusion.1), kind=kLoop, calls=%fused_computation.48 | loop fusion | flops 196608 | bytes 1179660 | tf_op jit(solution)/shard_map/jit(_where)/select_n | solution.py:268
  208.9 2.3 %copy.107 = bf16[12,2,2,64,64]{4,3,2,1,0:T(8,128)(2,1)} copy(bf16[12,2,2,64,64]{3,4,1,2,0:T(8,128)(2,1)} %bitcast_select_fusion) | data formatting | bytes 786432
  211.2 1.8 fusion.42
  (107 shorter events, 28.7 us)
Async XLA Ops:
  0.6 116.8 %copy-start = (bf16[384,1536]{1,0:T(8,128)(2,1)S(1)}, bf16[384,1536]{1,0:T(8,128)(2,1)}, u32[]{:S(2)}) copy-start(bf16[384,1536]{1,0:T(8,128)(2,1)} %param.23) | copy-start | bytes 3538948
  3.1 10.0 %collective-permute-start = (bf16[128,1536]{1,0:T(8,128)(2,1)S(1)}, bf16[128,1536]{1,0:T(8,128)(2,1)S(1)}, u32[]{:S(2)}, u32[]{:S(2)}) collective-permute-start(bf16[128,1536]{1,0:T(8,128)(2,1)S(1)} %fusion.41), channel_id=1, source_target_pairs={{0,2},{1,3},{2,0},{3,1},{4,6},{5,7},{6,4},{7,5},{8,10},{9,11},{10,... | collective-permute-start | bytes 1179656 | tf_op jit(solution)/shard_map/ppermute | solution.py:84
  5.6 10.2 %all-to-all-start = ((s32[32,1,128]{2,1,0:T(1,128)}), s32[32,1,128]{2,1,0:T(1,128)S(1)}, u32[]{:S(2)}, u32[]{:S(2)}) async-start(s32[32,1,128]{2,1,0:T(1,128)} %broadcast_in_dim.43), calls=%async_computation | async-start | bytes 32768 | tf_op jit(solution)/shard_map/all_to_all | solution.py:55
  13.2 5.0 %collective-permute-start.1 = (bf16[2,128,1536]{2,1,0:T(8,128)(2,1)S(1)}, bf16[2,128,1536]{2,1,0:T(8,128)(2,1)}, u32[]{:S(2)}, u32[]{:S(2)}) collective-permute-start(bf16[2,128,1536]{2,1,0:T(8,128)(2,1)S(1)} %get-tuple-element.32), channel_id=1, source_target_pairs={{0,1},{1,0},{2,3},{3,2},{4,5},{5,4},{6,7},{7,6},{8,9},{9,8},{10,11... | collective-permute-start | bytes 2359304 | tf_op jit(solution)/shard_map/ppermute | solution.py:86
  19.8 2.1 copy-start.18
  19.8 2.1 copy-start.19
  25.1 1.1 copy-start.10
  25.1 1.3 copy-start.12
  25.1 1.3 copy-start.13
  28.1 50.4 %all-to-all-start.1 = ((bf16[8,4,64,512]{3,2,1,0:T(8,128)(2,1)}), bf16[8,4,64,512]{3,2,1,0:T(8,128)(2,1)S(1)}, u32[]{:S(2)}, u32[]{:S(2)}) async-start(bf16[8,4,64,512]{3,2,1,0:T(8,128)(2,1)} %broadcast_in_dim.49), calls=%async_computation.1 | async-start | bytes 4194304 | tf_op jit(solution)/shard_map/all_to_all | solution.py:251
  78.5 1.4 copy-start.2
  119.6 1.2 copy-start.4
  120.8 3.4 %collective-permute-start.2 = (bf16[2,128,1536]{2,1,0:T(8,128)(2,1)S(1)}, bf16[2,128,1536]{2,1,0:T(8,128)(2,1)S(1)}, u32[]{:S(2)}, u32[]{:S(2)}) collective-permute-start(bf16[2,128,1536]{2,1,0:T(8,128)(2,1)S(1)} %select_bitcast_fusion.1), channel_id=1, source_target_pairs={{0,1},{1,0},{2,3},{3,2},{4,5},{5,4},{6,7},{7,6},{8,9},{9,8},{10,11... | collective-permute-start | bytes 2359304 | tf_op jit(solution)/shard_map/ppermute | solution.py:105
  122.4 14.0 %copy-start.6 = (bf16[128,1536]{1,0:T(8,128)(2,1)S(1)}, bf16[128,1536]{1,0:T(8,128)(2,1)}, u32[]{:S(2)}) copy-start(bf16[128,1536]{1,0:T(8,128)(2,1)} %param.14) | copy-start | bytes 1179652
  125.9 10.8 %copy-start.14 = (f32[1536]{0:T(1024)S(1)}, f32[1536]{0:T(1024)}, u32[]{:S(2)}) copy-start(f32[1536]{0:T(1024)} %param.19) | copy-start | bytes 18436
  126.0 10.4 %collective-permute-start.3 = (bf16[128,1536]{1,0:T(8,128)(2,1)S(1)}, bf16[128,1536]{1,0:T(8,128)(2,1)S(1)}, u32[]{:S(2)}, u32[]{:S(2)}) collective-permute-start(bf16[128,1536]{1,0:T(8,128)(2,1)S(1)} %fusion.43), channel_id=1, source_target_pairs={{0,2},{1,3},{2,0},{3,1},{4,6},{5,7},{6,4},{7,5},{8,10},{9,11},{10,... | collective-permute-start | bytes 1179656 | tf_op jit(solution)/shard_map/ppermute | solution.py:110
  136.7 1.3 copy-start.15
  136.7 1.3 copy-start.16
  137.7 9.4 %collective-permute-start.4 = (bf16[128,1536]{1,0:T(8,128)(2,1)S(1)}, bf16[128,1536]{1,0:T(8,128)(2,1)S(1)}, u32[]{:S(2)}, u32[]{:S(2)}) collective-permute-start(bf16[128,1536]{1,0:T(8,128)(2,1)S(1)} %get-tuple-element.25), channel_id=1, source_target_pairs={{0,2},{1,3},{2,0},{3,1},{4,6},{5,7},{6,4},{7,5},{8,10},{9,11},{10,... | collective-permute-start | bytes 1179656 | tf_op jit(solution)/shard_map/ppermute | solution.py:84
  138.6 11.2 %all-to-all-start.2 = ((f32[4,128,40]{1,2,0:T(8,128)}), f32[4,128,40]{1,2,0:T(8,128)S(1)}, u32[]{:S(2)}, u32[]{:S(2)}) async-start(f32[4,128,40]{1,2,0:T(8,128)} %broadcast_in_dim.53), calls=%async_computation.2 | async-start | bytes 163840 | tf_op jit(solution)/shard_map/all_to_all | solution.py:55
  147.2 4.5 %collective-permute-start.5 = (bf16[2,128,1536]{2,1,0:T(8,128)(2,1)S(1)}, bf16[2,128,1536]{2,1,0:T(8,128)(2,1)S(1)}, u32[]{:S(2)}, u32[]{:S(2)}) collective-permute-start(bf16[2,128,1536]{2,1,0:T(8,128)(2,1)S(1)} %get-tuple-element.30), channel_id=1, source_target_pairs={{0,1},{1,0},{2,3},{3,2},{4,5},{5,4},{6,7},{7,6},{8,9},{9,8},{10,11... | collective-permute-start | bytes 2359304 | tf_op jit(solution)/shard_map/ppermute | solution.py:86
  185.7 2.9 %copy-start.5 = (bf16[512,1536]{1,0:T(8,128)(2,1)}, bf16[512,1536]{1,0:T(8,128)(2,1)S(1)}, u32[]{:S(2)}) copy-start(bf16[512,1536]{1,0:T(8,128)(2,1)S(1)} %fusion.18) | copy-start | bytes 4718596
  185.7 1.7 copy-start.11
  185.7 2.9 %copy-start.17 = (s32[64]{0:T(128)S(1)}, s32[64]{0:T(128)}, u32[]{:S(2)}) copy-start(s32[64]{0:T(128)} %param.27) | copy-start | bytes 772
  185.8 3.5 %collective-permute-start.6 = (bf16[2,128,1536]{2,1,0:T(8,128)(2,1)S(1)}, bf16[2,128,1536]{2,1,0:T(8,128)(2,1)}, u32[]{:S(2)}, u32[]{:S(2)}) collective-permute-start(bf16[2,128,1536]{2,1,0:T(8,128)(2,1)S(1)} %select_bitcast_fusion), channel_id=1, source_target_pairs={{0,1},{1,0},{2,3},{3,2},{4,5},{5,4},{6,7},{7,6},{8,9},{9,8},{10,11... | collective-permute-start | bytes 2359304 | tf_op jit(solution)/shard_map/ppermute | solution.py:105
  189.3 4.5 %copy-start.3 = (bf16[8,4,64,512]{3,2,1,0:T(8,128)(2,1)S(1)}, bf16[8,4,64,512]{3,2,1,0:T(8,128)(2,1)}, u32[]{:S(2)}) copy-start(bf16[8,4,64,512]{3,2,1,0:T(8,128)(2,1)} %copy-done.2) | copy-start | bytes 6291460
  191.4 1.2 copy-start.7
  193.3 17.9 %collective-permute-start.7 = (bf16[128,1536]{1,0:T(8,128)(2,1)}, bf16[128,1536]{1,0:T(8,128)(2,1)}, u32[]{:S(2)}, u32[]{:S(2)}) collective-permute-start(bf16[128,1536]{1,0:T(8,128)(2,1)} %fusion.44), channel_id=1, source_target_pairs={{0,2},{1,3},{2,0},{3,1},{4,6},{5,7},{6,4},{7,5},{8,10},{9,11},{10,... | collective-permute-start | bytes 1179656 | tf_op jit(solution)/shard_map/ppermute | solution.py:110
  202.8 3.8 %copy-start.9 = (bf16[12,2,2,64,64]{3,4,1,2,0:T(8,128)(2,1)S(1)}, bf16[12,2,2,64,64]{3,4,1,2,0:T(8,128)(2,1)}, u32[]{:S(2)}) copy-start(bf16[12,2,2,64,64]{3,4,1,2,0:T(8,128)(2,1)} %copy.106) | copy-start | bytes 1179652
  206.6 4.6 %copy-start.8 = (f32[2,128,1536]{2,1,0:T(8,128)S(1)}, f32[2,128,1536]{2,1,0:T(8,128)}, u32[]{:S(2)}) copy-start(f32[2,128,1536]{2,1,0:T(8,128)} %copy-done.7) | copy-start | bytes 4718596
  206.6 6.4 %copy-start.1 = (bf16[384,1536]{1,0:T(8,128)(2,1)S(1)}, bf16[384,1536]{1,0:T(8,128)(2,1)}, u32[]{:S(2)}) copy-start(bf16[384,1536]{1,0:T(8,128)(2,1)} %param.23) | copy-start | bytes 3538948
